TPU v7x, 256 devices: a whole 4x4x8 slice. The times are simulated.
256 devices in a mesh: rep: 4 (over x), exp: 64 (over y, z, core).
Axes of the slice: x: 4, y: 4, z: 8, core: 2. Of those that a mesh axis runs over, the one named last changes fastest.
Arguments:
- tokens: bfloat16 [32768, 2048], P(('rep', 'exp')), may hold values from -6 to 6
- grad_out: bfloat16 [32768, 2048], P(('rep', 'exp')), may hold values from -6 to 6
- routes: int32 [32768, 2], P(('rep', 'exp')), may hold values from 0 to 63, all different within a row; in each aligned block of 128 rows (0 to 127, 128 to 255, ...) at most 8 rows name the same one
- gates: float32 [32768, 2], P(('rep', 'exp')), may hold values from 0.1 to 1
- w_gate: bfloat16 [64, 2048, 768], P('exp', 'rep'), may hold values from -0.125 to 0.125
- w_up: bfloat16 [64, 2048, 768], P('exp', 'rep'), may hold values from -0.125 to 0.125
- w_down: bfloat16 [64, 2048, 768], P('exp', 'rep'), may hold values from -0.125 to 0.125
Outputs:
- grad_gate: float32 [64, 2048, 768], P('exp', 'rep')
- grad_up: float32 [64, 2048, 768], P('exp', 'rep')
- grad_down: float32 [64, 2048, 768], P('exp', 'rep')
- grad_in: bfloat16 [32768, 2048], P(('rep', 'exp'))
Inputs may be any that keep to these rules, and one draw needn't show every extreme that they name: `routes`: each row names 2 different experts. Among the 128 rows of one device no expert is named more than 8 times, and in every draw some device names some expert exactly 8 times; every expert is named somewhere.
All inputs are finite; a program needn't handle non-finite values.
Results may differ from a plain program's by a relative error of at most 0.0065.
Values may be sent and summed in bfloat16 or wider, within the bound.
No kernel may reach another device: no remote copies, remote signals or barrier semaphores. Data moves between devices by JAX's collectives and lax.ppermute only.
A program may use at most 128 MiB of HBM per device.

v0:
```python
import jax
import jax.numpy as jnp
from jax import lax
from jax.sharding import PartitionSpec as P


def contract_rows(left, right):
    return lax.dot_general(
        left, right, (((0,), (0,)), ((), ())), preferred_element_type=jnp.float32
    )


def against_cols(left, right):
    return lax.dot_general(
        left, right, (((1,), (1,)), ((), ())), preferred_element_type=jnp.float32
    )


def per_device(tokens, grad_out, routes, gates, w_gate, w_up, w_down):
    tok_count, model_width = tokens.shape
    route_count = routes.shape[1]
    expert_count = lax.axis_size("exp")
    slot_cap = max(2, 2 * tok_count * route_count // expert_count)
    route_total = tok_count * route_count
    slot_total = expert_count * slot_cap
    flat_routes = routes.reshape(-1)
    onehot = (flat_routes[:, None] == jnp.arange(expert_count, dtype=jnp.int32)[None, :]).astype(
        jnp.int32
    )
    slot_rank = jnp.sum((jnp.cumsum(onehot, axis=0) - 1) * onehot, axis=1)
    slot_index = flat_routes * slot_cap + slot_rank
    source = (
        jnp.full((slot_total,), route_total, jnp.int32)
        .at[slot_index]
        .set(jnp.arange(route_total, dtype=jnp.int32))
    )
    scaled = (gates[:, :, None] * grad_out[:, None, :].astype(jnp.float32)).astype(jnp.bfloat16)
    scaled = scaled.reshape(route_total, model_width)
    zero_row = jnp.zeros((1, model_width), jnp.bfloat16)
    tok_pad = jnp.concatenate([tokens, zero_row], axis=0)
    scaled_pad = jnp.concatenate([scaled, zero_row], axis=0)
    tok_source = jnp.where(source < route_total, source // route_count, tok_count)
    x_send = tok_pad[tok_source]
    g_send = scaled_pad[source]
    x_recv, g_recv = (
        lax.all_to_all(x_send, "exp", split_axis=0, concat_axis=0, tiled=True),
        lax.all_to_all(g_send, "exp", split_axis=0, concat_axis=0, tiled=True),
    )
    full_gate, full_up, full_down = (
        lax.all_gather(w_gate[0], "rep", axis=0, tiled=True),
        lax.all_gather(w_up[0], "rep", axis=0, tiled=True),
        lax.all_gather(w_down[0], "rep", axis=0, tiled=True),
    )
    pre_gate = jnp.dot(x_recv, full_gate, preferred_element_type=jnp.float32)
    pre_up = jnp.dot(x_recv, full_up, preferred_element_type=jnp.float32)
    hid_grad = jnp.dot(g_recv, full_down, preferred_element_type=jnp.float32)
    sig_gate = jax.nn.sigmoid(pre_gate)
    silu_gate = pre_gate * sig_gate
    hidden = (silu_gate * pre_up).astype(jnp.bfloat16)
    d_gate = (hid_grad * pre_up * sig_gate * (1.0 + pre_gate * (1.0 - sig_gate))).astype(
        jnp.bfloat16
    )
    d_up = (hid_grad * silu_gate).astype(jnp.bfloat16)
    row_grad = (against_cols(d_gate, full_gate) + against_cols(d_up, full_up)).astype(jnp.bfloat16)
    returned = lax.all_to_all(row_grad, "exp", split_axis=0, concat_axis=0, tiled=True)
    picked = returned[slot_index].reshape(tok_count, route_count, model_width)
    grad_in = jnp.sum(picked.astype(jnp.float32), axis=1).astype(jnp.bfloat16)
    summed = lax.psum_scatter(
        jnp.stack(
            [
                contract_rows(x_recv, d_gate),
                contract_rows(x_recv, d_up),
                contract_rows(g_recv, hidden),
            ],
            axis=1,
        ),
        "rep",
        scatter_dimension=0,
        tiled=True,
    )
    grad_gate = summed[:, 0, :]
    grad_up = summed[:, 1, :]
    grad_down = summed[:, 2, :]
    return (grad_gate[None], grad_up[None], grad_down[None], grad_in)


def solution(mesh):
    placed = (
        P(("rep", "exp"), None),
        P(("rep", "exp"), None),
        P(("rep", "exp"), None),
        P(("rep", "exp"), None),
        P("exp", "rep", None),
        P("exp", "rep", None),
        P("exp", "rep", None),
    )
    return jax.shard_map(
        per_device,
        mesh=mesh,
        in_specs=placed,
        out_specs=(
            P("exp", "rep", None),
            P("exp", "rep", None),
            P("exp", "rep", None),
            P(("rep", "exp"), None),
        ),
        check_vma=False,
    )
```

profile of v0, /device:TPU:1, one launch (start us, length us, event | category | flops | bytes accessed | tf_op | source)
XLA Modules:
  0.0 344.5 jit_solution(4953015938019258746)
XLA Ops:
  7.2 0.0 all-gather.9.cloned.1.call-start
  7.2 0.7 all-gather.9.cloned.1.call-update
  7.9 0.0 all-gather.7.cloned.1.call-start
  8.0 0.7 all-gather.7.cloned.1.call-update
  8.7 0.7 broadcast_multiply_fusion
  9.3 0.8 copy.12
  10.1 0.1 eq.29
  10.3 0.1 eq.25
  10.4 0.1 copy.11
  10.5 0.1 mul.60
  10.7 0.6 reduce-window.6
  11.3 0.2 slice_reduce_fusion
  11.5 0.1 concatenate.6
  11.6 0.1 fusion.24
  11.7 1.4 scatter_custom_fusion
  13.1 3.3 gather_fusion
  16.5 13.5 %all-to-all-start = ((bf16[64,8,2048]{2,1,0:T(8,128)(2,1)}), bf16[64,8,2048]{2,1,0:T(8,128)(2,1)}, u32[]{:S(2)}, u32[]{:S(2)}) async-start(bf16[64,8,2048]{2,1,0:T(8,128)(2,1)} %bitcast.3), calls=%async_computation | async-start | bytes 4194304 | tf_op jit(solution)/shard_map/all_to_all | solution.py:46
  29.9 0.0 all-gather.11.cloned.1.call-start
  30.0 0.7 all-gather.11.cloned.1.call-update
  30.7 0.1 copy.15
  30.8 0.1 mul.62
  30.9 1.0 mul.64
  32.0 2.5 mul.65
  34.5 1.8 multiply_convert_fusion
  36.4 0.1 concatenate.7
  36.4 3.4 gather_fusion.1
  39.8 41.2 %all-to-all-done = bf16[64,8,2048]{2,1,0:T(8,128)(2,1)} async-done(((bf16[64,8,2048]{2,1,0:T(8,128)(2,1)}), bf16[64,8,2048]{2,1,0:T(8,128)(2,1)}, u32[]{:S(2)}, u32[]{:S(2)}) %all-to-all-start) | async-done | bytes 2097184 | tf_op jit(solution)/shard_map/all_to_all | solution.py:46
  81.1 5.8 %all-to-all-start.1 = ((bf16[64,8,2048]{2,1,0:T(8,128)(2,1)}), bf16[64,8,2048]{2,1,0:T(8,128)(2,1)S(1)}, u32[]{:S(2)}, u32[]{:S(2)}) async-start(bf16[64,8,2048]{2,1,0:T(8,128)(2,1)} %bitcast.5), calls=%async_computation.1 | async-start | bytes 4194304 | tf_op jit(solution)/shard_map/all_to_all | solution.py:47
  86.9 0.2 reduce-scatter.2.cloned.1.call-start
  87.2 5.5 %fusion.6 = f32[512,768]{1,0:T(8,128)} fusion(bf16[1,2048,768]{2,1,0:T(8,128)(2,1)} %all-gather.9.cloned.1.call-done, bf16[64,8,2048]{2,1,0:T(8,128)(2,1)} %all-to-all-done), kind=kOutput, calls=%fused_computation.15 | convolution fusion | flops 1610612736 | bytes 6815744 | tf_op jit(solution)/shard_map/dot_general | solution.py:55
  92.7 45.4 %all-to-all-done.1 = bf16[64,8,2048]{2,1,0:T(8,128)(2,1)S(1)} async-done(((bf16[64,8,2048]{2,1,0:T(8,128)(2,1)}), bf16[64,8,2048]{2,1,0:T(8,128)(2,1)S(1)}, u32[]{:S(2)}, u32[]{:S(2)}) %all-to-all-start.1) | async-done | bytes 2097184 | tf_op jit(solution)/shard_map/all_to_all | solution.py:47
  138.1 4.8 %fusion.8 = f32[512,768]{1,0:T(8,128)} fusion(bf16[1,2048,768]{2,1,0:T(8,128)(2,1)} %all-gather.7.cloned.1.call-done, bf16[64,8,2048]{2,1,0:T(8,128)(2,1)S(1)} %all-to-all-done.1), kind=kOutput, calls=%fused_computation.17 | convolution fusion | flops 1610612736 | bytes 6815744 | tf_op jit(solution)/shard_map/dot_general | solution.py:56
  142.9 0.7 all-gather.11.cloned.1.call-done
  143.6 5.8 %multiply_convert_fusion.3 = (bf16[512,768]{1,0:T(8,128)(2,1)S(1)}, bf16[512,768]{1,0:T(8,128)(2,1)S(1)}, f32[512,768]{1,0:T(8,128)S(1)}) fusion(f32[512,768]{1,0:T(8,128)} %fusion.8, f32[512,768]{1,0:T(8,128)} %fusion.6, bf16[1,2048,768]{2,1,0:T(8,128)(2,1)} %all-gather.11.cloned.1.call-done, bf16[64,8,2048]{2,1,0:T(8,128)(2,1)} %all-to-all-done), kind=kOutput, calls=%fused_computation.32 | convolution fusion | flops 1615724544 | bytes 11534336 | tf_op jit(solution)/shard_map/dot_general | solution.py:54
  149.5 2.0 convolution_bitcast_fusion
  151.5 3.5 %convolution_bitcast_fusion.1 = f32[2048,1,768]{2,0,1:T(8,128)S(1)} fusion(bf16[512,768]{1,0:T(8,128)(2,1)S(1)} %get-tuple-element.8, bf16[64,8,2048]{2,1,0:T(8,128)(2,1)} %all-to-all-done), kind=kOutput, calls=%fused_computation.7 | convolution fusion | flops 1610612736 | bytes 9175040 | tf_op jit(solution)/shard_map/dot_general | solution.py:8
  155.0 3.5 %convolution_bitcast_fusion.2 = f32[2048,1,768]{2,0,1:T(8,128)S(1)} fusion(bf16[512,768]{1,0:T(8,128)(2,1)S(1)} %get-tuple-element.7, bf16[64,8,2048]{2,1,0:T(8,128)(2,1)} %all-to-all-done), kind=kOutput, calls=%fused_computation.8 | convolution fusion | flops 1610612736 | bytes 9175040 | tf_op jit(solution)/shard_map/dot_general | solution.py:8
  158.5 6.9 %pad_maximum_fusion = f32[2048,3,768]{2,0,1:T(8,128)} fusion(f32[2048,1,768]{2,0,1:T(8,128)S(1)} %convolution_bitcast_fusion, f32[2048,1,768]{2,0,1:T(8,128)S(1)} %convolution_bitcast_fusion.1, f32[2048,1,768]{2,0,1:T(8,128)S(1)} %convolution_bitcast_fusion.2), kind=kLoop, calls=%fused_computation.4 | loop fusion | flops 9437184 | bytes 37748736 | tf_op jit(solution)/shard_map/stack | solution.py:69
  165.5 1.9 copy-done.4
  167.3 3.1 fusion
  170.5 3.2 fusion.12
  173.7 10.9 %all-to-all-start.2 = ((bf16[64,8,2048]{2,1,0:T(8,128)(2,1)}), bf16[64,8,2048]{2,1,0:T(8,128)(2,1)S(1)}, u32[]{:S(2)}, u32[]{:S(2)}) async-start(bf16[64,8,2048]{2,1,0:T(8,128)(2,1)} %fusion.12), calls=%async_computation.3 | async-start | bytes 4194304 | tf_op jit(solution)/shard_map/all_to_all | solution.py:65
  184.6 51.2 %all-to-all-done.2 = bf16[64,8,2048]{2,1,0:T(8,128)(2,1)S(1)} async-done(((bf16[64,8,2048]{2,1,0:T(8,128)(2,1)}), bf16[64,8,2048]{2,1,0:T(8,128)(2,1)S(1)}, u32[]{:S(2)}, u32[]{:S(2)}) %all-to-all-start.2) | async-done | bytes 2097184 | tf_op jit(solution)/shard_map/all_to_all | solution.py:65
  235.8 1.4 gather_fusion.2
  237.1 0.7 reshape.73
  237.9 3.7 %reduce_sum.25 = bf16[128,2048]{1,0:T(8,128)(2,1)} reduce(bf16[128,2,2048]{2,1,0:T(2,128)(2,1)S(1)} %reshape.73, bf16[]{:T(256)} %constant.13.clone.1), dimensions={1}, to_apply=%region_5.6 | reduce | flops 262144 | bytes 1572866 | tf_op jit(solution)/shard_map/reduce_sum | solution.py:67
  241.6 91.8 %reduce-scatter.2.cloned.1.call-done = f32[512,3,768]{2,0,1:T(8,128)} async-done(((f32[2048,3,768]{2,0,1:T(8,128)}), f32[512,3,768]{2,0,1:T(8,128)}) %reduce-scatter.2.cloned.1.call-update) | async-done | bytes 4718608 | tf_op jit(solution)/shard_map/reduce_scatter | solution.py:68
  333.3 4.6 %slice_bitcast_fusion = (f32[1,512,768]{2,1,0:T(8,128)}, f32[1,512,768]{2,1,0:T(8,128)}, f32[1,512,768]{2,1,0:T(8,128)}) fusion(f32[512,3,768]{2,0,1:T(8,128)} %reduce-scatter.2.cloned.1.call-done), kind=kLoop, calls=%fused_computation.27 | loop fusion | bytes 9437184 | tf_op jit(solution)/shard_map/broadcast_in_dim;squeeze | solution.py:84
  (28 shorter events, 0.2 us)
Async XLA Ops:
  7.2 4.4 %copy-start.1 = (bf16[128,2048]{1,0:T(8,128)(2,1)S(1)}, bf16[128,2048]{1,0:T(8,128)(2,1)}, u32[]{:S(2)}) copy-start(bf16[128,2048]{1,0:T(8,128)(2,1)} %param.7) | copy-start | bytes 1572868
  7.2 80.0 %all-gather.9.cloned.1.call-start = ((), (), s32[]{:S(2)}) async-start(), calls=%async_computation.6 | async-start | bytes 3932160 | tf_op jit(solution)/shard_map/all_gather | solution.py:51
  7.9 130.2 %all-gather.7.cloned.1.call-start = ((), (), s32[]{:S(2)}) async-start(), calls=%async_computation.5 | async-start | bytes 3932160 | tf_op jit(solution)/shard_map/all_gather | solution.py:52
  16.5 14.2 %copy-start.2 = (f32[128,2]{0,1:T(2,128)S(1)}, f32[128,2]{0,1:T(2,128)}, u32[]{:S(2)}) copy-start(f32[128,2]{0,1:T(2,128)} %param.10) | copy-start | bytes 3076
  16.5 14.5 %copy-start = (bf16[128,2048]{1,0:T(8,128)(2,1)S(1)}, bf16[128,2048]{1,0:T(8,128)(2,1)}, u32[]{:S(2)}) copy-start(bf16[128,2048]{1,0:T(8,128)(2,1)} %param.8) | copy-start | bytes 1572868
  16.5 64.6 %all-to-all-start = ((bf16[64,8,2048]{2,1,0:T(8,128)(2,1)}), bf16[64,8,2048]{2,1,0:T(8,128)(2,1)}, u32[]{:S(2)}, u32[]{:S(2)}) async-start(bf16[64,8,2048]{2,1,0:T(8,128)(2,1)} %bitcast.3), calls=%async_computation | async-start | bytes 4194304 | tf_op jit(solution)/shard_map/all_to_all | solution.py:46
  29.9 113.7 %all-gather.11.cloned.1.call-start = ((), (), s32[]{:S(2)}) async-start(), calls=%async_computation.7 | async-start | bytes 3932160 | tf_op jit(solution)/shard_map/all_gather | solution.py:50
  81.1 57.0 %all-to-all-start.1 = ((bf16[64,8,2048]{2,1,0:T(8,128)(2,1)}), bf16[64,8,2048]{2,1,0:T(8,128)(2,1)S(1)}, u32[]{:S(2)}, u32[]{:S(2)}) async-start(bf16[64,8,2048]{2,1,0:T(8,128)(2,1)} %bitcast.5), calls=%async_computation.1 | async-start | bytes 4194304 | tf_op jit(solution)/shard_map/all_to_all | solution.py:47
  86.9 246.4 %reduce-scatter.2.cloned.1.call-start = ((), (), s32[]{:S(2)}) async-start(), calls=%async_computation.4 | async-start | bytes 23592960 | tf_op jit(solution)/shard_map/reduce_scatter | solution.py:68
  143.6 5.8 %copy-start.8 = (f32[512,768]{1,0:T(8,128)S(1)}, f32[512,768]{1,0:T(8,128)}, u32[]{:S(2)}) copy-start(f32[512,768]{1,0:T(8,128)} %fusion.6) | copy-start | bytes 4718596
  149.4 2.1 copy-start.5
  149.4 5.6 %copy-start.7 = (bf16[512,768]{1,0:T(8,128)(2,1)}, bf16[512,768]{1,0:T(8,128)(2,1)S(1)}, u32[]{:S(2)}) copy-start(bf16[512,768]{1,0:T(8,128)(2,1)S(1)} %get-tuple-element.7) | copy-start | bytes 2359300
  165.4 1.9 copy-start.4
  167.3 3.1 copy-start.3
  167.3 3.1 copy-start.6
  173.7 62.1 %all-to-all-start.2 = ((bf16[64,8,2048]{2,1,0:T(8,128)(2,1)}), bf16[64,8,2048]{2,1,0:T(8,128)(2,1)S(1)}, u32[]{:S(2)}, u32[]{:S(2)}) async-start(bf16[64,8,2048]{2,1,0:T(8,128)(2,1)} %fusion.12), calls=%async_computation.3 | async-start | bytes 4194304 | tf_op jit(solution)/shard_map/all_to_all | solution.py:65
Sparse Core Ops, SparseCore 0:
  9.8 45.6 all-gather.8
  57.3 42.2 all-gather.6
  101.3 42.2 all-gather.10
  165.6 167.7 reduce-scatter.1
where the time goes:
time: 345 us
  waiting for transfers between devices  232 us (67%)
  matrix products  31.5 us (9%)
  starting transfers between devices  30.5 us (9%)
  local copies, waits for them, and re-layouts  22.2 us (6%)
  between operations  14 us (4%)
  other arithmetic  13.9 us (4%)
    reduce_scatter x1, waiting for transfers between devices, per_device(): lax.psum_scatter(jnp.stack([contract_rows(x_recv, d_gate), contract_rows(...  91.8 us
    all_to_all x1, waiting for transfers between devices, per_device(): lax.all_to_all(row_grad, 'exp', split_axis=0, concat_axis=0, tiled=True)  51.2 us
    all_to_all x1, waiting for transfers between devices, per_device(): lax.all_to_all(g_send, 'exp', split_axis=0, concat_axis=0, tiled=True)  45.4 us
    all_to_all x1, waiting for transfers between devices, per_device(): lax.all_to_all(x_send, 'exp', split_axis=0, concat_axis=0, tiled=True)  41.2 us
    all_to_all x1, starting transfers between devices, per_device(): lax.all_to_all(x_send, 'exp', split_axis=0, concat_axis=0, tiled=True)  13.5 us
    all_to_all x1, starting transfers between devices, per_device(): lax.all_to_all(row_grad, 'exp', split_axis=0, concat_axis=0, tiled=True)  10.9 us
    dot_general x3, matrix products, contract_rows(): lax.dot_general(left, right, (((0,), (0,)), ((), ())), preferred_element_...  9 us
    another operation x1, other arithmetic, per_device(): jnp.stack([contract_rows(x_recv, d_gate), contract_rows(x_recv, d_up), co...  6.93 us
  transfers between devices with their start and end apart: 7, of which 5 were waited for; matrix products, arithmetic and copies ran while one was open for 11% of the time, Pallas kernels for 0%

commit v1 on v0

--- a/solution.py
+++ b/solution.py
@@ -42,15 +42,15 @@
     tok_source = jnp.where(source < route_total, source // route_count, tok_count)
     x_send = tok_pad[tok_source]
     g_send = scaled_pad[source]
-    x_recv, g_recv = (
-        lax.all_to_all(x_send, "exp", split_axis=0, concat_axis=0, tiled=True),
-        lax.all_to_all(g_send, "exp", split_axis=0, concat_axis=0, tiled=True),
+    both_recv = lax.all_to_all(
+        jnp.concatenate([x_send, g_send], axis=1), "exp", split_axis=0, concat_axis=0, tiled=True
     )
-    full_gate, full_up, full_down = (
-        lax.all_gather(w_gate[0], "rep", axis=0, tiled=True),
-        lax.all_gather(w_up[0], "rep", axis=0, tiled=True),
-        lax.all_gather(w_down[0], "rep", axis=0, tiled=True),
+    x_recv = both_recv[:, :model_width]
+    g_recv = both_recv[:, model_width:]
+    full_all = lax.all_gather(
+        jnp.stack([w_gate[0], w_up[0], w_down[0]], axis=0), "rep", axis=1, tiled=True
     )
+    full_gate, full_up, full_down = full_all[0], full_all[1], full_all[2]
     pre_gate = jnp.dot(x_recv, full_gate, preferred_element_type=jnp.float32)
     pre_up = jnp.dot(x_recv, full_up, preferred_element_type=jnp.float32)
     hid_grad = jnp.dot(g_recv, full_down, preferred_element_type=jnp.float32)
@@ -73,11 +73,12 @@
                 contract_rows(g_recv, hidden),
             ],
             axis=1,
-        ),
+        ).astype(jnp.bfloat16),
         "rep",
         scatter_dimension=0,
         tiled=True,
     )
+    summed = summed.astype(jnp.float32)
     grad_gate = summed[:, 0, :]
     grad_up = summed[:, 1, :]
     grad_down = summed[:, 2, :]

time: 345 us -> 261 us (0.76)
  waiting for transfers between devices: 232 us -> 67.8 us
  blocking collectives: 0 us -> 109 us
  starting transfers between devices: 30.5 us -> 5.91 us
  matrix products: 31.5 us -> 26.7 us
  other arithmetic: 13.9 us -> 18.3 us
  local copies, waits for them, and re-layouts: 22.2 us -> 18.2 us
    all_to_all x0 -> x1, blocking collectives: none -> 109 us  [per_device(): lax.all_to_all(jnp.concatenate([x_send, g_send], axis=1), 'exp', split_ax...]
    all_to_all x2 -> x0, waiting for transfers between devices: 86.7 us -> none  [the longest x1 45.4 us: per_device(): lax.all_to_all(g_send, 'exp', split_axis=0, concat_axis=0, tiled=True)]
    reduce_scatter x1, waiting for transfers between devices: 91.8 us -> 16.5 us  [per_device(): lax.psum_scatter(jnp.stack([contract_rows(x_recv, d_gate), contract_rows(...]
    all_to_all x2 -> x0, starting transfers between devices: 19.3 us -> none  [the longest x1 13.5 us: per_device(): lax.all_to_all(x_send, 'exp', split_axis=0, concat_axis=0, tiled=True)]
    all_to_all x1, starting transfers between devices: 10.9 us -> 5.83 us  [per_device(): lax.all_to_all(row_grad, 'exp', split_axis=0, concat_axis=0, tiled=True)]
  transfers between devices with their start and end apart: 7 -> 3, of which waited for: 5 -> 2; matrix products, arithmetic and copies ran while one was open for 11% -> 12% of each run, Pallas kernels for 0% -> 0%
where the time goes in v1:
time: 261 us; the launch traced here: 260 us
  blocking collectives  109 us (42%)
  waiting for transfers between devices  67.8 us (26%)
  matrix products  26.7 us (10%)
  other arithmetic  18.3 us (7%)
  local copies, waits for them, and re-layouts  18.2 us (7%)
  between operations  14.3 us (5%)
  starting transfers between devices  5.91 us (2%)
    all_to_all x1, blocking collectives, per_device(): lax.all_to_all(jnp.concatenate([x_send, g_send], axis=1), 'exp', split_ax...  109 us
    all_to_all x1, waiting for transfers between devices, per_device(): lax.all_to_all(row_grad, 'exp', split_axis=0, concat_axis=0, tiled=True)  51.2 us
    reduce_scatter x1, waiting for transfers between devices, per_device(): lax.psum_scatter(jnp.stack([contract_rows(x_recv, d_gate), contract_rows(...  16.5 us
    dot_general x2, matrix products, against_cols(): lax.dot_general(left, right, (((1,), (1,)), ((), ())), preferred_element_...  8.81 us
    all_to_all x1, starting transfers between devices, per_device(): lax.all_to_all(row_grad, 'exp', split_axis=0, concat_axis=0, tiled=True)  5.83 us
    dot_general x3, matrix products, contract_rows(): lax.dot_general(left, right, (((0,), (0,)), ((), ())), preferred_element_...  5.62 us
  transfers between devices with their start and end apart: 3, of which 2 were waited for; matrix products, arithmetic and copies ran while one was open for 12% of the time, Pallas kernels for 0%

profile of v1, /device:TPU:1, one launch (start us, length us, event | category | flops | bytes accessed | tf_op | source)
XLA Modules:
  0.0 260.2 jit_solution(16459104574923453076)
XLA Ops:
  7.2 0.0 all-gather.2.cloned.1.call-start
  7.2 3.3 %pad_maximum_fusion.1 = bf16[3,512,768]{2,1,0:T(8,128)(2,1)} fusion(bf16[1,512,768]{2,1,0:T(8,128)(2,1)} %param.13, bf16[1,512,768]{2,1,0:T(8,128)(2,1)} %param.12, bf16[1,512,768]{2,1,0:T(8,128)(2,1)} %param.11), kind=kLoop, calls=%fused_computation.21 | loop fusion | flops 2359296 | bytes 4718592 | tf_op jit(solution)/shard_map/stack | solution.py:51
  10.5 0.0 all-gather.2.cloned.1.call-update
  10.5 0.0 reduce-scatter.2.cloned.1.call-start
  10.5 0.6 copy-done.5
  11.1 0.1 copy.12
  11.3 0.1 eq.29
  11.4 0.1 eq.25
  11.6 0.6 reduce-window.6
  12.2 0.2 slice_reduce_fusion
  12.4 0.1 copy.11
  12.5 0.1 mul.60
  12.7 1.0 mul.64
  13.7 0.0 copy-start.6
  13.7 2.4 mul.65
  16.2 0.0 copy-done.4
  16.2 0.1 copy.15
  16.3 0.1 mul.62
  16.4 0.0 copy-start.3
  16.5 1.8 multiply_convert_fusion
  18.3 0.0 slice-start
  18.3 0.1 concatenate.10
  18.4 0.1 concatenate.9
  18.5 0.5 slice-done
  19.0 0.1 fusion.17
  19.1 1.4 scatter_custom_fusion
  20.5 3.3 %gather_fusion.1 = bf16[512,2048]{1,0:T(8,128)(2,1)} fusion(bf16[257,2048]{1,0:T(8,128)(2,1)S(1)} %concatenate.10, s32[1024]{0:T(1024)S(1)} %get-tuple-element.12), kind=kCustom, calls=%fused_computation.1 | custom fusion | bytes 4196352 | tf_op jit(solution)/shard_map/gather | solution.py:44
  23.8 3.3 %gather_fusion = bf16[512,2048]{1,0:T(8,128)(2,1)} fusion(bf16[129,2048]{1,0:T(8,128)(2,1)S(1)} %concatenate.9, s32[1024]{0:T(1024)S(1)} %get-tuple-element.13), kind=kCustom, calls=%fused_computation | custom fusion | bytes 4196352 | tf_op jit(solution)/shard_map/gather | solution.py:43
  27.1 2.3 maximum_bitcast_fusion
  29.4 109.0 %all_to_all.24 = bf16[64,8,4096]{2,1,0:T(8,128)(2,1)} all-to-all(bf16[64,8,4096]{2,1,0:T(8,128)(2,1)S(1)} %maximum_bitcast_fusion), channel_id=1, replica_groups=mesh['rep'=4,'exp'=64] {'exp'}, dimensions={0} | all-to-all | bytes 8388608 | tf_op jit(solution)/shard_map/all_to_all | solution.py:45
  138.4 4.5 %fusion.4 = f32[512,768]{1,0:T(8,128)S(1)} fusion(bf16[3,2048,768]{2,1,0:T(8,128)(2,1)} %all-gather.2.cloned.1.call-done, bf16[512,4096]{1,0:T(8,128)(2,1)} %bitcast.55), kind=kOutput, calls=%fused_computation.17 | convolution fusion | flops 1610612736 | bytes 6815744 | tf_op jit(solution)/shard_map/dot_general | solution.py:55
  142.9 3.7 %fusion = f32[512,768]{1,0:T(8,128)S(1)} fusion(bf16[3,2048,768]{2,1,0:T(8,128)(2,1)} %all-gather.2.cloned.1.call-done, bf16[512,4096]{1,0:T(8,128)(2,1)S(1)} %bitcast.56), kind=kOutput, calls=%fused_computation.13 | convolution fusion | flops 1610612736 | bytes 6815744 | tf_op jit(solution)/shard_map/dot_general | solution.py:56
  146.6 4.1 %multiply_convert_fusion.3 = (bf16[512,768]{1,0:T(8,128)(2,1)S(1)}, bf16[512,768]{1,0:T(8,128)(2,1)S(1)}, f32[512,768]{1,0:T(8,128)S(1)}) fusion(f32[512,768]{1,0:T(8,128)S(1)} %fusion, f32[512,768]{1,0:T(8,128)S(1)} %fusion.4, bf16[3,2048,768]{2,1,0:T(8,128)(2,1)} %all-gather.2.cloned.1.call-done, bf16[512,4096]{1,0:T(8,128)(2,1)S(1)} %bitcast.57), kind=kOutput, calls=%fused_computation.30 | convolution fusion | flops 1615724544 | bytes 11534336 | tf_op jit(solution)/shard_map/dot_general | solution.py:54
  150.7 1.8 fusion.1
  152.6 1.8 fusion.2
  154.4 1.9 fusion.3
  156.4 4.5 %pad_maximum_fusion = bf16[2048,3,768]{2,0,1:T(8,128)(2,1)} fusion(bf16[2048,1,768]{2,0,1:T(8,128)(2,1)S(1)} %fusion.3, bf16[2048,1,768]{2,0,1:T(8,128)(2,1)S(1)} %fusion.2, bf16[2048,1,768]{2,0,1:T(8,128)(2,1)S(1)} %fusion.1), kind=kLoop, calls=%fused_computation.4 | loop fusion | flops 9437184 | bytes 18874368 | tf_op jit(solution)/shard_map/stack | solution.py:69
  160.9 0.0 reduce-scatter.2.cloned.1.call-update
  160.9 3.7 %fusion.5 = f32[512,2048]{1,0:T(8,128)S(1)} fusion(bf16[512,768]{1,0:T(8,128)(2,1)S(1)} %get-tuple-element.7, bf16[3,2048,768]{2,1,0:T(8,128)(2,1)} %all-gather.2.cloned.1.call-done), kind=kOutput, calls=%fused_computation.18 | convolution fusion | flops 1610612736 | bytes 8126464 | tf_op jit(solution)/shard_map/dot_general | solution.py:14
  164.6 5.1 %fusion.7 = bf16[64,8,2048]{2,1,0:T(8,128)(2,1)} fusion(f32[512,2048]{1,0:T(8,128)S(1)} %fusion.5, bf16[512,768]{1,0:T(8,128)(2,1)S(1)} %get-tuple-element.8, bf16[3,2048,768]{2,1,0:T(8,128)(2,1)} %all-gather.2.cloned.1.call-done), kind=kOutput, calls=%fused_computation.20 | convolution fusion | flops 1612709888 | bytes 10223616 | tf_op jit(solution)/shard_map/dot_general | solution.py:14
  169.7 5.8 %all-to-all-start.1 = ((bf16[64,8,2048]{2,1,0:T(8,128)(2,1)}), bf16[64,8,2048]{2,1,0:T(8,128)(2,1)S(1)}, u32[]{:S(2)}, u32[]{:S(2)}) async-start(bf16[64,8,2048]{2,1,0:T(8,128)(2,1)} %fusion.7), calls=%async_computation.2 | async-start | bytes 4194304 | tf_op jit(solution)/shard_map/all_to_all | solution.py:65
  175.6 51.2 %all-to-all-done.1 = bf16[64,8,2048]{2,1,0:T(8,128)(2,1)S(1)} async-done(((bf16[64,8,2048]{2,1,0:T(8,128)(2,1)}), bf16[64,8,2048]{2,1,0:T(8,128)(2,1)S(1)}, u32[]{:S(2)}, u32[]{:S(2)}) %all-to-all-start.1) | async-done | bytes 2097184 | tf_op jit(solution)/shard_map/all_to_all | solution.py:65
  226.8 1.4 gather_fusion.2
  228.1 0.7 reshape.71
  228.8 3.6 %reduce_sum.25 = bf16[128,2048]{1,0:T(8,128)(2,1)} reduce(bf16[128,2,2048]{2,1,0:T(2,128)(2,1)S(1)} %reshape.71, bf16[]{:T(256)} %constant.13.clone.1), dimensions={1}, to_apply=%region_5.6 | reduce | flops 262144 | bytes 1572866 | tf_op jit(solution)/shard_map/reduce_sum | solution.py:67
  232.5 16.5 %reduce-scatter.2.cloned.1.call-done = bf16[512,3,768]{2,0,1:T(8,128)(2,1)} async-done(((bf16[2048,3,768]{2,0,1:T(8,128)(2,1)}), bf16[512,3,768]{2,0,1:T(8,128)(2,1)}) %reduce-scatter.2.cloned.1.call-update) | async-done | bytes 2359312 | tf_op jit(solution)/shard_map/reduce_scatter | solution.py:68
  249.0 2.1 convert_element_type.37
  251.1 2.3 slice_bitcast_fusion.10
  (19 shorter events, 0.1 us)
Async XLA Ops:
  7.2 131.3 %all-gather.2.cloned.1.call-start = ((), (), s32[]{:S(2)}) async-start(), calls=%async_computation.3 | async-start | bytes 11796480 | tf_op jit(solution)/shard_map/all_gather | solution.py:50
  10.5 0.7 copy-start.5
  10.5 2.2 copy-start.2
  10.5 238.5 %reduce-scatter.2.cloned.1.call-start = ((), (), s32[]{:S(2)}) async-start(), calls=%async_computation.4 | async-start | bytes 11796480 | tf_op jit(solution)/shard_map/reduce_scatter | solution.py:68
  12.4 3.8 %copy-start.4 = (s32[64,3]{0,1:T(4,128)}, s32[64,3]{0,1:T(4,128)S(1)}, u32[]{:S(2)}) copy-start(s32[64,3]{0,1:T(4,128)S(1)} %reduce-window.9) | copy-start | bytes 2308
  13.7 2.5 copy-start.6
  16.4 2.0 copy-start.3
  18.3 0.7 slice-start
  23.8 3.3 %copy-start = (bf16[512,2048]{1,0:T(8,128)(2,1)S(1)}, bf16[512,2048]{1,0:T(8,128)(2,1)}, u32[]{:S(2)}) copy-start(bf16[512,2048]{1,0:T(8,128)(2,1)} %gather_fusion.1) | copy-start | bytes 6291460
  138.4 4.5 %copy-start.1 = (bf16[64,8,4096]{2,1,0:T(8,128)(2,1)S(1)}, bf16[64,8,4096]{2,1,0:T(8,128)(2,1)}, u32[]{:S(2)}) copy-start(bf16[64,8,4096]{2,1,0:T(8,128)(2,1)} %all_to_all.24) | copy-start | bytes 12582916
  169.7 57.0 %all-to-all-start.1 = ((bf16[64,8,2048]{2,1,0:T(8,128)(2,1)}), bf16[64,8,2048]{2,1,0:T(8,128)(2,1)S(1)}, u32[]{:S(2)}, u32[]{:S(2)}) async-start(bf16[64,8,2048]{2,1,0:T(8,128)(2,1)} %fusion.7), calls=%async_computation.2 | async-start | bytes 4194304 | tf_op jit(solution)/shard_map/all_to_all | solution.py:65
Sparse Core Ops, SparseCore 0:
  10.6 98.0 all-gather.1
  161.0 87.9 reduce-scatter.1

commit v2 on v1

--- a/solution.py
+++ b/solution.py
@@ -35,16 +35,15 @@
         .set(jnp.arange(route_total, dtype=jnp.int32))
     )
     scaled = (gates[:, :, None] * grad_out[:, None, :].astype(jnp.float32)).astype(jnp.bfloat16)
-    scaled = scaled.reshape(route_total, model_width)
-    zero_row = jnp.zeros((1, model_width), jnp.bfloat16)
-    tok_pad = jnp.concatenate([tokens, zero_row], axis=0)
-    scaled_pad = jnp.concatenate([scaled, zero_row], axis=0)
-    tok_source = jnp.where(source < route_total, source // route_count, tok_count)
-    x_send = tok_pad[tok_source]
-    g_send = scaled_pad[source]
-    both_recv = lax.all_to_all(
-        jnp.concatenate([x_send, g_send], axis=1), "exp", split_axis=0, concat_axis=0, tiled=True
-    )
+    table = jnp.concatenate(
+        [
+            jnp.broadcast_to(tokens[:, None, :], (tok_count, route_count, model_width)),
+            scaled,
+        ],
+        axis=2,
+    ).reshape(route_total, 2 * model_width)
+    table = jnp.concatenate([table, jnp.zeros((1, 2 * model_width), jnp.bfloat16)], axis=0)
+    both_recv = lax.all_to_all(table[source], "exp", split_axis=0, concat_axis=0, tiled=True)
     x_recv = both_recv[:, :model_width]
     g_recv = both_recv[:, model_width:]
     full_all = lax.all_gather(
@@ -72,16 +71,16 @@
                 contract_rows(x_recv, d_up),
                 contract_rows(g_recv, hidden),
             ],
-            axis=1,
+            axis=0,
         ).astype(jnp.bfloat16),
         "rep",
-        scatter_dimension=0,
+        scatter_dimension=1,
         tiled=True,
     )
     summed = summed.astype(jnp.float32)
-    grad_gate = summed[:, 0, :]
-    grad_up = summed[:, 1, :]
-    grad_down = summed[:, 2, :]
+    grad_gate = summed[0]
+    grad_up = summed[1]
+    grad_down = summed[2]
     return (grad_gate[None], grad_up[None], grad_down[None], grad_in)
 
 

time: 261 us -> 257 us (0.985)
  other arithmetic: 18.3 us -> 12.6 us
    slice x1 -> x2, local copies, waits for them, and re-layouts: 0.18 us -> 4.08 us  [the longest x1 3.89 us: per_device(): grad_down = summed[2]]
    another operation x3 -> x2, local copies, waits for them, and re-layouts: 2.77 us -> 0.01 us  [the longest x1 2.28 us: per_device(): return (grad_gate[None], grad_up[None], grad_down[None], grad_in)]
    gather x2 -> x1, local copies, waits for them, and re-layouts: 6.62 us -> 4.37 us  [per_device(): table[source]]
  transfers between devices with their start and end apart: 3 -> 3, of which waited for: 2 -> 2; matrix products, arithmetic and copies ran while one was open for 12% -> 11% of each run, Pallas kernels for 0% -> 0%
where the time goes in v2:
time: 257 us
  blocking collectives  109 us (42%)
  waiting for transfers between devices  67.8 us (26%)
  matrix products  26.7 us (10%)
  local copies, waits for them, and re-layouts  20 us (8%)
  between operations  14.3 us (6%)
  other arithmetic  12.6 us (5%)
  starting transfers between devices  5.9 us (2%)
    all_to_all x1, blocking collectives, per_device(): lax.all_to_all(table[source], 'exp', split_axis=0, concat_axis=0, tiled=T...  109 us
    all_to_all x1, waiting for transfers between devices, per_device(): lax.all_to_all(row_grad, 'exp', split_axis=0, concat_axis=0, tiled=True)  51.2 us
    reduce_scatter x1, waiting for transfers between devices, per_device(): lax.psum_scatter(jnp.stack([contract_rows(x_recv, d_gate), contract_rows(...  16.6 us
    dot_general x2, matrix products, against_cols(): lax.dot_general(left, right, (((1,), (1,)), ((), ())), preferred_element_...  8.82 us
    all_to_all x1, starting transfers between devices, per_device(): lax.all_to_all(row_grad, 'exp', split_axis=0, concat_axis=0, tiled=True)  5.82 us
    dot_general x3, matrix products, contract_rows(): lax.dot_general(left, right, (((0,), (0,)), ((), ())), preferred_element_...  5.62 us
  transfers between devices with their start and end apart: 3, of which 2 were waited for; matrix products, arithmetic and copies ran while one was open for 11% of the time, Pallas kernels for 0%

profile of v2, /device:TPU:1, one launch (start us, length us, event | category | flops | bytes accessed | tf_op | source)
XLA Modules:
  0.0 256.6 jit_solution(11965757812897440927)
XLA Ops:
  7.2 0.0 all-gather.2.cloned.1.call-start
  7.2 3.3 %pad_maximum_fusion.1 = bf16[3,512,768]{2,1,0:T(8,128)(2,1)} fusion(bf16[1,512,768]{2,1,0:T(8,128)(2,1)} %param.13, bf16[1,512,768]{2,1,0:T(8,128)(2,1)} %param.12, bf16[1,512,768]{2,1,0:T(8,128)(2,1)} %param.11), kind=kLoop, calls=%fused_computation.22 | loop fusion | flops 2359296 | bytes 4718592 | tf_op jit(solution)/shard_map/stack | solution.py:50
  10.5 0.0 all-gather.2.cloned.1.call-update
  10.5 0.0 reduce-scatter.2.cloned.1.call-start
  10.6 0.6 copy-done.5
  11.2 0.1 copy.13
  11.3 0.1 eq.29
  11.4 0.1 eq.25
  11.6 0.6 reduce-window.6
  12.2 0.2 slice_reduce_fusion
  12.4 0.1 copy.12
  12.5 0.1 mul.65
  12.7 0.0 copy-done.3
  12.7 1.0 mul.60
  13.7 0.0 copy-start.6
  13.7 2.4 mul.61
  16.2 0.0 copy-done.4
  16.2 0.0 copy-done.6
  16.2 0.1 copy.11
  16.3 0.1 mul.58
  16.5 1.8 broadcast_in_dim.6
  18.3 1.2 concatenate.9
  19.5 0.0 slice-done
  19.5 0.1 fusion.20
  19.6 1.4 scatter_custom_fusion
  21.0 0.0 copy-done
  21.1 0.2 multiply_convert_fusion
  21.2 0.0 copy-done.2
  21.2 0.2 fusion.10
  21.5 4.4 %gather_fusion = bf16[512,4096]{1,0:T(8,128)(2,1)} fusion(bf16[257,4096]{1,0:T(8,128)(2,1)S(1)} %fusion.10, s32[1024]{0:T(1024)S(1)} %pad_clamp_fusion.1), kind=kCustom, calls=%fused_computation | custom fusion | bytes 8390656 | tf_op jit(solution)/shard_map/gather | solution.py:46
  25.8 109.4 %all_to_all.24 = bf16[64,8,4096]{2,1,0:T(8,128)(2,1)} all-to-all(bf16[64,8,4096]{2,1,0:T(8,128)(2,1)} %bitcast.48), channel_id=1, replica_groups=mesh['rep'=4,'exp'=64] {'exp'}, dimensions={0} | all-to-all | bytes 8388608 | tf_op jit(solution)/shard_map/all_to_all | solution.py:46
  135.2 4.5 %fusion.6 = f32[512,768]{1,0:T(8,128)S(1)} fusion(bf16[3,2048,768]{2,1,0:T(8,128)(2,1)} %all-gather.2.cloned.1.call-done, bf16[512,4096]{1,0:T(8,128)(2,1)} %bitcast.49), kind=kOutput, calls=%fused_computation.18 | convolution fusion | flops 1610612736 | bytes 6815744 | tf_op jit(solution)/shard_map/dot_general | solution.py:54
  139.7 3.7 %fusion.2 = f32[512,768]{1,0:T(8,128)S(1)} fusion(bf16[3,2048,768]{2,1,0:T(8,128)(2,1)} %all-gather.2.cloned.1.call-done, bf16[512,4096]{1,0:T(8,128)(2,1)S(1)} %bitcast.50), kind=kOutput, calls=%fused_computation.14 | convolution fusion | flops 1610612736 | bytes 6815744 | tf_op jit(solution)/shard_map/dot_general | solution.py:55
  143.4 4.1 %multiply_convert_fusion.3 = (bf16[512,768]{1,0:T(8,128)(2,1)S(1)}, bf16[512,768]{1,0:T(8,128)(2,1)S(1)}, f32[512,768]{1,0:T(8,128)S(1)}) fusion(f32[512,768]{1,0:T(8,128)S(1)} %fusion.2, f32[512,768]{1,0:T(8,128)S(1)} %fusion.6, bf16[3,2048,768]{2,1,0:T(8,128)(2,1)} %all-gather.2.cloned.1.call-done, bf16[512,4096]{1,0:T(8,128)(2,1)S(1)} %bitcast.51), kind=kOutput, calls=%fused_computation.29 | convolution fusion | flops 1615724544 | bytes 11534336 | tf_op jit(solution)/shard_map/dot_general | solution.py:53
  147.5 1.9 fusion.5
  149.5 1.8 fusion.3
  151.3 1.8 fusion.4
  153.2 4.5 %pad_maximum_fusion = bf16[3,2048,768]{2,1,0:T(8,128)(2,1)} fusion(bf16[1,2048,768]{2,1,0:T(8,128)(2,1)S(1)} %fusion.5, bf16[1,2048,768]{2,1,0:T(8,128)(2,1)S(1)} %fusion.4, bf16[1,2048,768]{2,1,0:T(8,128)(2,1)S(1)} %fusion.3), kind=kLoop, calls=%fused_computation.3 | loop fusion | flops 9437184 | bytes 18874368 | tf_op jit(solution)/shard_map/stack | solution.py:68
  157.7 0.0 reduce-scatter.2.cloned.1.call-update
  157.7 3.7 %fusion.7 = f32[512,2048]{1,0:T(8,128)S(1)} fusion(bf16[512,768]{1,0:T(8,128)(2,1)S(1)} %get-tuple-element.4, bf16[3,2048,768]{2,1,0:T(8,128)(2,1)} %all-gather.2.cloned.1.call-done), kind=kOutput, calls=%fused_computation.19 | convolution fusion | flops 1610612736 | bytes 8126464 | tf_op jit(solution)/shard_map/dot_general | solution.py:14
  161.4 5.1 %fusion.9 = bf16[64,8,2048]{2,1,0:T(8,128)(2,1)} fusion(f32[512,2048]{1,0:T(8,128)S(1)} %fusion.7, bf16[512,768]{1,0:T(8,128)(2,1)S(1)} %get-tuple-element.5, bf16[3,2048,768]{2,1,0:T(8,128)(2,1)} %all-gather.2.cloned.1.call-done), kind=kOutput, calls=%fused_computation.21 | convolution fusion | flops 1612709888 | bytes 10223616 | tf_op jit(solution)/shard_map/dot_general | solution.py:14
  166.5 5.8 %all-to-all-start.1 = ((bf16[64,8,2048]{2,1,0:T(8,128)(2,1)}), bf16[64,8,2048]{2,1,0:T(8,128)(2,1)S(1)}, u32[]{:S(2)}, u32[]{:S(2)}) async-start(bf16[64,8,2048]{2,1,0:T(8,128)(2,1)} %fusion.9), calls=%async_computation.2 | async-start | bytes 4194304 | tf_op jit(solution)/shard_map/all_to_all | solution.py:64
  172.4 51.2 %all-to-all-done.1 = bf16[64,8,2048]{2,1,0:T(8,128)(2,1)S(1)} async-done(((bf16[64,8,2048]{2,1,0:T(8,128)(2,1)}), bf16[64,8,2048]{2,1,0:T(8,128)(2,1)S(1)}, u32[]{:S(2)}, u32[]{:S(2)}) %all-to-all-start.1) | async-done | bytes 2097184 | tf_op jit(solution)/shard_map/all_to_all | solution.py:64
  223.5 1.4 gather_fusion.1
  224.9 0.7 reshape.74
  225.6 3.6 %reduce_sum.25 = bf16[128,2048]{1,0:T(8,128)(2,1)} reduce(bf16[128,2,2048]{2,1,0:T(2,128)(2,1)S(1)} %reshape.74, bf16[]{:T(256)} %constant.8.clone.1), dimensions={1}, to_apply=%region_5.6 | reduce | flops 262144 | bytes 1572866 | tf_op jit(solution)/shard_map/reduce_sum | solution.py:66
  229.3 16.6 %reduce-scatter.2.cloned.1.call-done = bf16[3,512,768]{2,1,0:T(8,128)(2,1)} async-done(((bf16[3,2048,768]{2,1,0:T(8,128)(2,1)}), bf16[3,512,768]{2,1,0:T(8,128)(2,1)}) %reduce-scatter.2.cloned.1.call-update) | async-done | bytes 2359312 | tf_op jit(solution)/shard_map/reduce_scatter | solution.py:67
  245.8 3.9 %fusion.25 = (f32[1,512,768]{2,1,0:T(8,128)}, f32[1,512,768]{2,1,0:T(8,128)}, f32[1,512,768]{2,1,0:T(8,128)}) fusion(bf16[3,512,768]{2,1,0:T(8,128)(2,1)} %reduce-scatter.2.cloned.1.call-done), kind=kLoop, calls=%fused_computation.52 | loop fusion | bytes 9437184 | tf_op jit(solution)/shard_map/slice | solution.py:83
  (17 shorter events, 0.1 us)
Async XLA Ops:
  7.2 128.1 %all-gather.2.cloned.1.call-start = ((), (), s32[]{:S(2)}) async-start(), calls=%async_computation.3 | async-start | bytes 11796480 | tf_op jit(solution)/shard_map/all_gather | solution.py:49
  10.5 0.7 copy-start.5
  10.5 2.2 copy-start.3
  10.5 235.3 %reduce-scatter.2.cloned.1.call-start = ((), (), s32[]{:S(2)}) async-start(), calls=%async_computation.4 | async-start | bytes 11796480 | tf_op jit(solution)/shard_map/reduce_scatter | solution.py:67
  12.4 3.8 %copy-start.4 = (s32[64,3]{0,1:T(4,128)}, s32[64,3]{0,1:T(4,128)S(1)}, u32[]{:S(2)}) copy-start(s32[64,3]{0,1:T(4,128)S(1)} %reduce-window.9) | copy-start | bytes 2308
  13.7 2.5 copy-start.6
  16.2 4.8 %copy-start = (f32[256,2048]{1,0:T(8,128)S(1)}, f32[256,2048]{1,0:T(8,128)}, u32[]{:S(2)}) copy-start(f32[256,2048]{1,0:T(8,128)} %mul.61) | copy-start | bytes 6291460
  16.3 3.2 %slice-start = ((s32[64,3]{0,1:T(4,128)}), s32[64,2]{0,1:T(2,128)S(1)}, s32[]{:S(2)}) async-start(s32[64,3]{0,1:T(4,128)} %copy-done.4), calls=%async_computation.5 | async-start | bytes 2048 | tf_op jit(solution)/shard_map/slice.1
  19.5 1.7 copy-start.2
  135.2 4.5 %copy-start.1 = (bf16[64,8,4096]{2,1,0:T(8,128)(2,1)S(1)}, bf16[64,8,4096]{2,1,0:T(8,128)(2,1)}, u32[]{:S(2)}) copy-start(bf16[64,8,4096]{2,1,0:T(8,128)(2,1)} %all_to_all.24) | copy-start | bytes 12582916
  166.5 57.0 %all-to-all-start.1 = ((bf16[64,8,2048]{2,1,0:T(8,128)(2,1)}), bf16[64,8,2048]{2,1,0:T(8,128)(2,1)S(1)}, u32[]{:S(2)}, u32[]{:S(2)}) async-start(bf16[64,8,2048]{2,1,0:T(8,128)(2,1)} %fusion.9), calls=%async_computation.2 | async-start | bytes 4194304 | tf_op jit(solution)/shard_map/all_to_all | solution.py:64
Sparse Core Ops, SparseCore 0:
  10.6 98.0 all-gather.1
  157.8 87.9 reduce-scatter.1

commit v3 on v2

--- a/solution.py
+++ b/solution.py
@@ -34,16 +34,19 @@
         .at[slot_index]
         .set(jnp.arange(route_total, dtype=jnp.int32))
     )
-    scaled = (gates[:, :, None] * grad_out[:, None, :].astype(jnp.float32)).astype(jnp.bfloat16)
-    table = jnp.concatenate(
-        [
-            jnp.broadcast_to(tokens[:, None, :], (tok_count, route_count, model_width)),
-            scaled,
-        ],
-        axis=2,
-    ).reshape(route_total, 2 * model_width)
-    table = jnp.concatenate([table, jnp.zeros((1, 2 * model_width), jnp.bfloat16)], axis=0)
-    both_recv = lax.all_to_all(table[source], "exp", split_axis=0, concat_axis=0, tiled=True)
+    tok_source = jnp.where(source < route_total, source // route_count, tok_count)
+    pair_rows = jnp.concatenate(
+        [jnp.concatenate([tokens, grad_out], axis=1), jnp.zeros((1, 2 * model_width), jnp.bfloat16)],
+        axis=0,
+    )[tok_source]
+    gate_of = jnp.concatenate([gates.reshape(-1), jnp.zeros((1,), gates.dtype)])[source]
+    row_scale = jnp.where(
+        jnp.arange(2 * model_width)[None, :] < model_width, jnp.ones((), gates.dtype), gate_of[:, None]
+    )
+    send = (pair_rows.astype(jnp.float32) * row_scale).astype(jnp.bfloat16)
+    both_recv = lax.all_to_all(
+        send.reshape(slot_total, 2 * model_width), "exp", split_axis=0, concat_axis=0, tiled=True
+    )
     x_recv = both_recv[:, :model_width]
     g_recv = both_recv[:, model_width:]
     full_all = lax.all_gather(

time: 257 us -> 258 us (level)
  other arithmetic: 12.6 us -> 16 us
  local copies, waits for them, and re-layouts: 20 us -> 17.1 us
    mul x3 -> x0, local copies, waits for them, and re-layouts: 3.62 us -> none  [per_device(): gates[:, :, None] * grad_out[:, None, :].astype(jnp.float32)]
    gather x1 -> x2, local copies, waits for them, and re-layouts: 4.37 us -> 7.97 us  [the longest x1 4.48 us: per_device(): jnp.concatenate([jnp.concatenate([tokens, grad_out], axis=1), jnp.zeros((...]
    convert_element_type x1, other arithmetic: 0.18 us -> 3.68 us  [per_device(): send = (pair_rows.astype(jnp.float32) * row_scale).astype(jnp.bfloat16)]
  transfers between devices with their start and end apart: 3 -> 3, of which waited for: 2 -> 2; matrix products, arithmetic and copies ran while one was open for 11% -> 12% of each run, Pallas kernels for 0% -> 0%
where the time goes in v3:
time: 258 us; the launch traced here: 257 us
  blocking collectives  110 us (43%)
  waiting for transfers between devices  67.8 us (26%)
  matrix products  26.7 us (10%)
  local copies, waits for them, and re-layouts  17.1 us (7%)
  other arithmetic  16 us (6%)
  between operations  14.3 us (6%)
  starting transfers between devices  5.9 us (2%)
    all_to_all x1, blocking collectives, per_device(): lax.all_to_all(send.reshape(slot_total, 2 * model_width), 'exp', split_ax...  110 us
    all_to_all x1, waiting for transfers between devices, per_device(): lax.all_to_all(row_grad, 'exp', split_axis=0, concat_axis=0, tiled=True)  51.2 us
    reduce_scatter x1, waiting for transfers between devices, per_device(): lax.psum_scatter(jnp.stack([contract_rows(x_recv, d_gate), contract_rows(...  16.5 us
    dot_general x2, matrix products, against_cols(): lax.dot_general(left, right, (((1,), (1,)), ((), ())), preferred_element_...  8.81 us
    all_to_all x1, starting transfers between devices, per_device(): lax.all_to_all(row_grad, 'exp', split_axis=0, concat_axis=0, tiled=True)  5.82 us
    dot_general x3, matrix products, contract_rows(): lax.dot_general(left, right, (((0,), (0,)), ((), ())), preferred_element_...  5.62 us
  transfers between devices with their start and end apart: 3, of which 2 were waited for; matrix products, arithmetic and copies ran while one was open for 12% of the time, Pallas kernels for 0%

profile of v3, /device:TPU:1, one launch (start us, length us, event | category | flops | bytes accessed | tf_op | source)
XLA Modules:
  0.0 257.5 jit_solution(11383803817276660140)
XLA Ops:
  7.2 0.0 all-gather.2.cloned.1.call-start
  7.2 3.2 %pad_maximum_fusion.1 = bf16[3,512,768]{2,1,0:T(8,128)(2,1)} fusion(bf16[1,512,768]{2,1,0:T(8,128)(2,1)} %param.13, bf16[1,512,768]{2,1,0:T(8,128)(2,1)} %param.12, bf16[1,512,768]{2,1,0:T(8,128)(2,1)} %param.11), kind=kLoop, calls=%fused_computation.22 | loop fusion | flops 2359296 | bytes 4718592 | tf_op jit(solution)/shard_map/stack | solution.py:53
  10.5 0.0 copy-start.3
  10.5 0.0 copy-start.4
  10.5 0.0 copy-start.1
  10.5 0.0 copy-start.2
  10.5 0.0 all-gather.2.cloned.1.call-update
  10.5 0.0 reduce-scatter.2.cloned.1.call-start
  10.5 0.6 copy-done.3
  11.1 0.1 copy.12
  11.3 0.1 eq.29
  11.4 0.1 eq.25
  11.6 0.6 reduce-window.6
  12.2 0.2 slice_reduce_fusion
  12.4 0.1 copy.11
  12.5 0.1 mul.46
  12.7 0.0 copy-done.4
  12.7 0.1 copy.15
  12.8 0.1 reshape.86
  12.9 0.1 fusion.21
  13.0 1.4 scatter_custom_fusion
  14.5 3.5 %gather_fusion.1 = f32[512]{0:T(512)S(1)} fusion(f32[257]{0:T(512)S(1)} %pad_maximum_fusion.2, s32[1024]{0:T(1024)S(1)} %get-tuple-element.12), kind=kCustom, calls=%fused_computation.1 | custom fusion | bytes 6144 | tf_op jit(solution)/shard_map/gather | solution.py:42
  18.0 0.1 broadcast_in_dim.43
  18.1 0.0 copy-done.1
  18.1 0.0 copy-done.2
  18.1 0.1 fusion.18
  18.2 4.5 %gather_fusion = bf16[512,4096]{1,0:T(8,128)(2,1)} fusion(bf16[129,4096]{1,0:T(8,128)(2,1)S(1)} %fusion.18, s32[1024]{0:T(1024)S(1)} %get-tuple-element.13), kind=kCustom, calls=%fused_computation | custom fusion | bytes 8390656 | tf_op jit(solution)/shard_map/gather | solution.py:38
  22.7 3.7 %fusion = bf16[64,8,4096]{2,1,0:T(8,128)(2,1)S(1)} fusion(bf16[512,4096]{1,0:T(8,128)(2,1)} %gather_fusion, f32[64,8]{1,0:T(8,128)S(1)} %broadcast_in_dim.43, pred[4096]{0:T(1024)(128)(4,1)S(1)} %iota_compare_fusion.3), kind=kLoop, calls=%fused_computation.6 | loop fusion | flops 8388608 | bytes 8394752 | tf_op jit(solution)/shard_map/convert_element_type | solution.py:46
  26.4 109.8 %all_to_all.21 = bf16[64,8,4096]{2,1,0:T(8,128)(2,1)} all-to-all(bf16[64,8,4096]{2,1,0:T(8,128)(2,1)S(1)} %fusion), channel_id=1, replica_groups=mesh['rep'=4,'exp'=64] {'exp'}, dimensions={0} | all-to-all | bytes 8388608 | tf_op jit(solution)/shard_map/all_to_all | solution.py:47
  136.2 0.0 all-gather.2.cloned.1.call-done
  136.2 4.5 %fusion.5 = f32[512,768]{1,0:T(8,128)S(1)} fusion(bf16[3,2048,768]{2,1,0:T(8,128)(2,1)} %all-gather.2.cloned.1.call-done, bf16[512,4096]{1,0:T(8,128)(2,1)} %bitcast.50), kind=kOutput, calls=%fused_computation.18 | convolution fusion | flops 1610612736 | bytes 6815744 | tf_op jit(solution)/shard_map/dot_general | solution.py:57
  140.6 0.0 copy-done
  140.7 3.7 %fusion.1 = f32[512,768]{1,0:T(8,128)S(1)} fusion(bf16[3,2048,768]{2,1,0:T(8,128)(2,1)} %all-gather.2.cloned.1.call-done, bf16[512,4096]{1,0:T(8,128)(2,1)S(1)} %bitcast.51), kind=kOutput, calls=%fused_computation.14 | convolution fusion | flops 1610612736 | bytes 6815744 | tf_op jit(solution)/shard_map/dot_general | solution.py:58
  144.3 4.1 %multiply_convert_fusion.2 = (bf16[512,768]{1,0:T(8,128)(2,1)S(1)}, bf16[512,768]{1,0:T(8,128)(2,1)S(1)}, f32[512,768]{1,0:T(8,128)S(1)}) fusion(f32[512,768]{1,0:T(8,128)S(1)} %fusion.1, f32[512,768]{1,0:T(8,128)S(1)} %fusion.5, bf16[3,2048,768]{2,1,0:T(8,128)(2,1)} %all-gather.2.cloned.1.call-done, bf16[512,4096]{1,0:T(8,128)(2,1)S(1)} %bitcast.52), kind=kOutput, calls=%fused_computation.30 | convolution fusion | flops 1615724544 | bytes 11534336 | tf_op jit(solution)/shard_map/dot_general | solution.py:56
  148.5 1.8 fusion.2
  150.3 1.8 fusion.3
  152.2 1.9 fusion.4
  154.1 4.5 %pad_maximum_fusion = bf16[3,2048,768]{2,1,0:T(8,128)(2,1)} fusion(bf16[1,2048,768]{2,1,0:T(8,128)(2,1)S(1)} %fusion.4, bf16[1,2048,768]{2,1,0:T(8,128)(2,1)S(1)} %fusion.3, bf16[1,2048,768]{2,1,0:T(8,128)(2,1)S(1)} %fusion.2), kind=kLoop, calls=%fused_computation.4 | loop fusion | flops 9437184 | bytes 18874368 | tf_op jit(solution)/shard_map/stack | solution.py:71
  158.6 0.0 reduce-scatter.2.cloned.1.call-update
  158.6 3.7 %fusion.6 = f32[512,2048]{1,0:T(8,128)S(1)} fusion(bf16[512,768]{1,0:T(8,128)(2,1)S(1)} %get-tuple-element.4, bf16[3,2048,768]{2,1,0:T(8,128)(2,1)} %all-gather.2.cloned.1.call-done), kind=kOutput, calls=%fused_computation.19 | convolution fusion | flops 1610612736 | bytes 8126464 | tf_op jit(solution)/shard_map/dot_general | solution.py:14
  162.4 5.1 %fusion.8 = bf16[64,8,2048]{2,1,0:T(8,128)(2,1)} fusion(f32[512,2048]{1,0:T(8,128)S(1)} %fusion.6, bf16[512,768]{1,0:T(8,128)(2,1)S(1)} %get-tuple-element.5, bf16[3,2048,768]{2,1,0:T(8,128)(2,1)} %all-gather.2.cloned.1.call-done), kind=kOutput, calls=%fused_computation.21 | convolution fusion | flops 1612709888 | bytes 10223616 | tf_op jit(solution)/shard_map/dot_general | solution.py:14
  167.5 5.8 %all-to-all-start.1 = ((bf16[64,8,2048]{2,1,0:T(8,128)(2,1)}), bf16[64,8,2048]{2,1,0:T(8,128)(2,1)S(1)}, u32[]{:S(2)}, u32[]{:S(2)}) async-start(bf16[64,8,2048]{2,1,0:T(8,128)(2,1)} %fusion.8), calls=%async_computation.2 | async-start | bytes 4194304 | tf_op jit(solution)/shard_map/all_to_all | solution.py:67
  173.3 51.2 %all-to-all-done.1 = bf16[64,8,2048]{2,1,0:T(8,128)(2,1)S(1)} async-done(((bf16[64,8,2048]{2,1,0:T(8,128)(2,1)}), bf16[64,8,2048]{2,1,0:T(8,128)(2,1)S(1)}, u32[]{:S(2)}, u32[]{:S(2)}) %all-to-all-start.1) | async-done | bytes 2097184 | tf_op jit(solution)/shard_map/all_to_all | solution.py:67
  224.5 1.4 gather_fusion.2
  225.8 0.7 reshape.87
  226.6 3.6 %reduce_sum.25 = bf16[128,2048]{1,0:T(8,128)(2,1)} reduce(bf16[128,2,2048]{2,1,0:T(2,128)(2,1)S(1)} %reshape.87, bf16[]{:T(256)} %constant.13.clone.1), dimensions={1}, to_apply=%region_5.6 | reduce | flops 262144 | bytes 1572866 | tf_op jit(solution)/shard_map/reduce_sum | solution.py:69
  230.2 16.5 %reduce-scatter.2.cloned.1.call-done = bf16[3,512,768]{2,1,0:T(8,128)(2,1)} async-done(((bf16[3,2048,768]{2,1,0:T(8,128)(2,1)}), bf16[3,512,768]{2,1,0:T(8,128)(2,1)}) %reduce-scatter.2.cloned.1.call-update) | async-done | bytes 2359312 | tf_op jit(solution)/shard_map/reduce_scatter | solution.py:70
  246.8 3.9 %fusion.29 = (f32[1,512,768]{2,1,0:T(8,128)}, f32[1,512,768]{2,1,0:T(8,128)}, f32[1,512,768]{2,1,0:T(8,128)}) fusion(bf16[3,512,768]{2,1,0:T(8,128)(2,1)} %reduce-scatter.2.cloned.1.call-done), kind=kLoop, calls=%fused_computation.66 | loop fusion | bytes 9437184 | tf_op jit(solution)/shard_map/slice | solution.py:86
  (12 shorter events, 0.1 us)
Async XLA Ops:
  7.2 129.0 %all-gather.2.cloned.1.call-start = ((), (), s32[]{:S(2)}) async-start(), calls=%async_computation.3 | async-start | bytes 11796480 | tf_op jit(solution)/shard_map/all_gather | solution.py:52
  10.5 0.7 copy-start.3
  10.5 2.2 copy-start.4
  10.5 7.6 %copy-start.1 = (bf16[128,2048]{1,0:T(8,128)(2,1)S(1)}, bf16[128,2048]{1,0:T(8,128)(2,1)}, u32[]{:S(2)}) copy-start(bf16[128,2048]{1,0:T(8,128)(2,1)} %param.8) | copy-start | bytes 1572868
  10.5 7.6 %copy-start.2 = (bf16[128,2048]{1,0:T(8,128)(2,1)S(1)}, bf16[128,2048]{1,0:T(8,128)(2,1)}, u32[]{:S(2)}) copy-start(bf16[128,2048]{1,0:T(8,128)(2,1)} %param.7) | copy-start | bytes 1572868
  10.5 236.3 %reduce-scatter.2.cloned.1.call-start = ((), (), s32[]{:S(2)}) async-start(), calls=%async_computation.4 | async-start | bytes 11796480 | tf_op jit(solution)/shard_map/reduce_scatter | solution.py:70
  136.2 4.5 %copy-start = (bf16[64,8,4096]{2,1,0:T(8,128)(2,1)S(1)}, bf16[64,8,4096]{2,1,0:T(8,128)(2,1)}, u32[]{:S(2)}) copy-start(bf16[64,8,4096]{2,1,0:T(8,128)(2,1)} %all_to_all.21) | copy-start | bytes 12582916
  167.5 57.0 %all-to-all-start.1 = ((bf16[64,8,2048]{2,1,0:T(8,128)(2,1)}), bf16[64,8,2048]{2,1,0:T(8,128)(2,1)S(1)}, u32[]{:S(2)}, u32[]{:S(2)}) async-start(bf16[64,8,2048]{2,1,0:T(8,128)(2,1)} %fusion.8), calls=%async_computation.2 | async-start | bytes 4194304 | tf_op jit(solution)/shard_map/all_to_all | solution.py:67
Sparse Core Ops, SparseCore 0:
  10.6 98.0 all-gather.1
  158.8 87.9 reduce-scatter.1

commit v4 on v2

--- a/solution.py
+++ b/solution.py
@@ -34,16 +34,26 @@
         .at[slot_index]
         .set(jnp.arange(route_total, dtype=jnp.int32))
     )
-    scaled = (gates[:, :, None] * grad_out[:, None, :].astype(jnp.float32)).astype(jnp.bfloat16)
     table = jnp.concatenate(
         [
-            jnp.broadcast_to(tokens[:, None, :], (tok_count, route_count, model_width)),
-            scaled,
-        ],
-        axis=2,
-    ).reshape(route_total, 2 * model_width)
-    table = jnp.concatenate([table, jnp.zeros((1, 2 * model_width), jnp.bfloat16)], axis=0)
-    both_recv = lax.all_to_all(table[source], "exp", split_axis=0, concat_axis=0, tiled=True)
+            jnp.concatenate(
+                [
+                    tokens,
+                    (gates[:, k : k + 1] * grad_out.astype(jnp.float32)).astype(jnp.bfloat16),
+                ],
+                axis=1,
+            )
+            for k in range(route_count)
+        ]
+        + [jnp.zeros((1, 2 * model_width), jnp.bfloat16)],
+        axis=0,
+    )
+    by_choice = jnp.where(
+        source < route_total,
+        (source % route_count) * tok_count + source // route_count,
+        route_total,
+    )
+    both_recv = lax.all_to_all(table[by_choice], "exp", split_axis=0, concat_axis=0, tiled=True)
     x_recv = both_recv[:, :model_width]
     g_recv = both_recv[:, model_width:]
     full_all = lax.all_gather(

time: 257 us -> 250 us (0.973)
  local copies, waits for them, and re-layouts: 20 us -> 12.6 us
    mul x3 -> x1, local copies, waits for them, and re-layouts: 3.62 us -> 0.01 us  [per_device(): gates[:, k:k + 1] * grad_out.astype(jnp.float32)]
  transfers between devices with their start and end apart: 3 -> 3, of which waited for: 2 -> 2; matrix products, arithmetic and copies ran while one was open for 11% -> 9% of each run, Pallas kernels for 0% -> 0%
where the time goes in v4:
time: 250 us
  blocking collectives  109 us (44%)
  waiting for transfers between devices  67.8 us (27%)
  matrix products  26.7 us (11%)
  between operations  14.3 us (6%)
  other arithmetic  13.1 us (5%)
  local copies, waits for them, and re-layouts  12.6 us (5%)
  starting transfers between devices  5.91 us (2%)
    all_to_all x1, blocking collectives, per_device(): lax.all_to_all(table[by_choice], 'exp', split_axis=0, concat_axis=0, tile...  109 us
    all_to_all x1, waiting for transfers between devices, per_device(): lax.all_to_all(row_grad, 'exp', split_axis=0, concat_axis=0, tiled=True)  51.2 us
    reduce_scatter x1, waiting for transfers between devices, per_device(): lax.psum_scatter(jnp.stack([contract_rows(x_recv, d_gate), contract_rows(...  16.5 us
    dot_general x2, matrix products, against_cols(): lax.dot_general(left, right, (((1,), (1,)), ((), ())), preferred_element_...  8.82 us
    all_to_all x1, starting transfers between devices, per_device(): lax.all_to_all(row_grad, 'exp', split_axis=0, concat_axis=0, tiled=True)  5.83 us
    dot_general x3, matrix products, contract_rows(): lax.dot_general(left, right, (((0,), (0,)), ((), ())), preferred_element_...  5.62 us
  transfers between devices with their start and end apart: 3, of which 2 were waited for; matrix products, arithmetic and copies ran while one was open for 9% of the time, Pallas kernels for 0%

profile of v4, /device:TPU:1, one launch (start us, length us, event | category | flops | bytes accessed | tf_op | source)
XLA Modules:
  0.0 249.7 jit_solution(16537512083927101329)
XLA Ops:
  7.2 0.0 copy-start.3
  7.2 0.0 copy-start.4
  7.2 0.0 copy-start.1
  7.2 0.0 all-gather.2.cloned.1.call-start
  7.2 3.3 %pad_maximum_fusion.1 = bf16[3,512,768]{2,1,0:T(8,128)(2,1)} fusion(bf16[1,512,768]{2,1,0:T(8,128)(2,1)} %param.13, bf16[1,512,768]{2,1,0:T(8,128)(2,1)} %param.12, bf16[1,512,768]{2,1,0:T(8,128)(2,1)} %param.11), kind=kLoop, calls=%fused_computation.19 | loop fusion | flops 2359296 | bytes 4718592 | tf_op jit(solution)/shard_map/stack | solution.py:60
  10.6 0.0 copy-start.2
  10.6 0.0 all-gather.2.cloned.1.call-update
  10.6 0.0 reduce-scatter.2.cloned.1.call-start
  10.6 0.0 copy-done.3
  10.6 0.1 copy.12
  10.8 0.1 eq.31
  10.9 0.1 eq.27
  11.1 0.6 reduce-window.6
  11.7 0.2 slice_reduce_fusion
  11.9 0.1 copy.11
  12.0 0.1 mul.74
  12.2 0.1 fusion.19
  12.3 1.4 scatter_custom_fusion
  13.7 0.0 copy-done.4
  13.8 0.0 copy-done.1
  13.8 0.2 fusion.15
  14.0 0.0 copy-done.2
  14.0 0.6 maximum_maximum_fusion
  14.6 4.4 %gather_fusion = bf16[512,4096]{1,0:T(8,128)(2,1)} fusion(bf16[257,4096]{1,0:T(8,128)(2,1)S(1)} %maximum_maximum_fusion, s32[1024]{0:T(1024)S(1)} %pad_clamp_fusion.1), kind=kCustom, calls=%fused_computation | custom fusion | bytes 8390656 | tf_op jit(solution)/shard_map/gather | solution.py:56
  19.0 109.4 %all_to_all.24 = bf16[64,8,4096]{2,1,0:T(8,128)(2,1)} all-to-all(bf16[64,8,4096]{2,1,0:T(8,128)(2,1)} %bitcast.53), channel_id=1, replica_groups=mesh['rep'=4,'exp'=64] {'exp'}, dimensions={0} | all-to-all | bytes 8388608 | tf_op jit(solution)/shard_map/all_to_all | solution.py:56
  128.4 0.0 all-gather.2.cloned.1.call-done
  128.4 0.0 copy-start
  128.4 4.5 %fusion.4 = f32[512,768]{1,0:T(8,128)S(1)} fusion(bf16[3,2048,768]{2,1,0:T(8,128)(2,1)} %all-gather.2.cloned.1.call-done, bf16[512,4096]{1,0:T(8,128)(2,1)} %bitcast.54), kind=kOutput, calls=%fused_computation.15 | convolution fusion | flops 1610612736 | bytes 6815744 | tf_op jit(solution)/shard_map/dot_general | solution.py:64
  132.8 0.0 copy-done
  132.9 3.7 %fusion = f32[512,768]{1,0:T(8,128)S(1)} fusion(bf16[3,2048,768]{2,1,0:T(8,128)(2,1)} %all-gather.2.cloned.1.call-done, bf16[512,4096]{1,0:T(8,128)(2,1)S(1)} %bitcast.55), kind=kOutput, calls=%fused_computation.11 | convolution fusion | flops 1610612736 | bytes 6815744 | tf_op jit(solution)/shard_map/dot_general | solution.py:65
  136.5 4.1 %multiply_convert_fusion.2 = (bf16[512,768]{1,0:T(8,128)(2,1)S(1)}, bf16[512,768]{1,0:T(8,128)(2,1)S(1)}, f32[512,768]{1,0:T(8,128)S(1)}) fusion(f32[512,768]{1,0:T(8,128)S(1)} %fusion, f32[512,768]{1,0:T(8,128)S(1)} %fusion.4, bf16[3,2048,768]{2,1,0:T(8,128)(2,1)} %all-gather.2.cloned.1.call-done, bf16[512,4096]{1,0:T(8,128)(2,1)S(1)} %bitcast.56), kind=kOutput, calls=%fused_computation.25 | convolution fusion | flops 1615724544 | bytes 11534336 | tf_op jit(solution)/shard_map/dot_general | solution.py:63
  140.7 1.8 fusion.1
  142.5 1.8 fusion.2
  144.4 1.9 fusion.3
  146.3 4.5 %pad_maximum_fusion = bf16[3,2048,768]{2,1,0:T(8,128)(2,1)} fusion(bf16[1,2048,768]{2,1,0:T(8,128)(2,1)S(1)} %fusion.3, bf16[1,2048,768]{2,1,0:T(8,128)(2,1)S(1)} %fusion.2, bf16[1,2048,768]{2,1,0:T(8,128)(2,1)S(1)} %fusion.1), kind=kLoop, calls=%fused_computation.3 | loop fusion | flops 9437184 | bytes 18874368 | tf_op jit(solution)/shard_map/stack | solution.py:78
  150.8 0.0 reduce-scatter.2.cloned.1.call-update
  150.8 3.7 %fusion.5 = f32[512,2048]{1,0:T(8,128)S(1)} fusion(bf16[512,768]{1,0:T(8,128)(2,1)S(1)} %get-tuple-element.4, bf16[3,2048,768]{2,1,0:T(8,128)(2,1)} %all-gather.2.cloned.1.call-done), kind=kOutput, calls=%fused_computation.16 | convolution fusion | flops 1610612736 | bytes 8126464 | tf_op jit(solution)/shard_map/dot_general | solution.py:14
  154.6 5.1 %fusion.7 = bf16[64,8,2048]{2,1,0:T(8,128)(2,1)} fusion(f32[512,2048]{1,0:T(8,128)S(1)} %fusion.5, bf16[512,768]{1,0:T(8,128)(2,1)S(1)} %get-tuple-element.5, bf16[3,2048,768]{2,1,0:T(8,128)(2,1)} %all-gather.2.cloned.1.call-done), kind=kOutput, calls=%fused_computation.18 | convolution fusion | flops 1612709888 | bytes 10223616 | tf_op jit(solution)/shard_map/dot_general | solution.py:14
  159.7 5.8 %all-to-all-start.1 = ((bf16[64,8,2048]{2,1,0:T(8,128)(2,1)}), bf16[64,8,2048]{2,1,0:T(8,128)(2,1)S(1)}, u32[]{:S(2)}, u32[]{:S(2)}) async-start(bf16[64,8,2048]{2,1,0:T(8,128)(2,1)} %fusion.7), calls=%async_computation.2 | async-start | bytes 4194304 | tf_op jit(solution)/shard_map/all_to_all | solution.py:74
  165.5 51.2 %all-to-all-done.1 = bf16[64,8,2048]{2,1,0:T(8,128)(2,1)S(1)} async-done(((bf16[64,8,2048]{2,1,0:T(8,128)(2,1)}), bf16[64,8,2048]{2,1,0:T(8,128)(2,1)S(1)}, u32[]{:S(2)}, u32[]{:S(2)}) %all-to-all-start.1) | async-done | bytes 2097184 | tf_op jit(solution)/shard_map/all_to_all | solution.py:74
  216.7 1.4 gather_fusion.1
  218.1 0.7 reshape.64
  218.8 3.6 %reduce_sum.25 = bf16[128,2048]{1,0:T(8,128)(2,1)} reduce(bf16[128,2,2048]{2,1,0:T(2,128)(2,1)S(1)} %reshape.64, bf16[]{:T(256)} %constant.41.clone.1), dimensions={1}, to_apply=%region_5.6 | reduce | flops 262144 | bytes 1572866 | tf_op jit(solution)/shard_map/reduce_sum | solution.py:76
  222.4 16.5 %reduce-scatter.2.cloned.1.call-done = bf16[3,512,768]{2,1,0:T(8,128)(2,1)} async-done(((bf16[3,2048,768]{2,1,0:T(8,128)(2,1)}), bf16[3,512,768]{2,1,0:T(8,128)(2,1)}) %reduce-scatter.2.cloned.1.call-update) | async-done | bytes 2359312 | tf_op jit(solution)/shard_map/reduce_scatter | solution.py:77
  238.9 3.9 %fusion.29 = (f32[1,512,768]{2,1,0:T(8,128)}, f32[1,512,768]{2,1,0:T(8,128)}, f32[1,512,768]{2,1,0:T(8,128)}) fusion(bf16[3,512,768]{2,1,0:T(8,128)(2,1)} %reduce-scatter.2.cloned.1.call-done), kind=kLoop, calls=%fused_computation.65 | loop fusion | bytes 9437184 | tf_op jit(solution)/shard_map/slice | solution.py:93
  (11 shorter events, 0.1 us)
Async XLA Ops:
  7.2 3.5 %copy-start.3 = (s32[128,2]{0,1:T(2,128)S(1)}, s32[128,2]{0,1:T(2,128)}, u32[]{:S(2)}) copy-start(s32[128,2]{0,1:T(2,128)} %param.9) | copy-start | bytes 3076
  7.2 6.6 %copy-start.4 = (f32[128,2]{0,1:T(2,128)S(1)}, f32[128,2]{0,1:T(2,128)}, u32[]{:S(2)}) copy-start(f32[128,2]{0,1:T(2,128)} %param.10) | copy-start | bytes 3076
  7.2 6.6 %copy-start.1 = (bf16[128,2048]{1,0:T(8,128)(2,1)S(1)}, bf16[128,2048]{1,0:T(8,128)(2,1)}, u32[]{:S(2)}) copy-start(bf16[128,2048]{1,0:T(8,128)(2,1)} %param.8) | copy-start | bytes 1572868
  7.2 121.2 %all-gather.2.cloned.1.call-start = ((), (), s32[]{:S(2)}) async-start(), calls=%async_computation.3 | async-start | bytes 11796480 | tf_op jit(solution)/shard_map/all_gather | solution.py:59
  10.6 3.5 %copy-start.2 = (bf16[128,2048]{1,0:T(8,128)(2,1)S(1)}, bf16[128,2048]{1,0:T(8,128)(2,1)}, u32[]{:S(2)}) copy-start(bf16[128,2048]{1,0:T(8,128)(2,1)} %param.7) | copy-start | bytes 1572868
  10.6 228.4 %reduce-scatter.2.cloned.1.call-start = ((), (), s32[]{:S(2)}) async-start(), calls=%async_computation.4 | async-start | bytes 11796480 | tf_op jit(solution)/shard_map/reduce_scatter | solution.py:77
  128.4 4.5 %copy-start = (bf16[64,8,4096]{2,1,0:T(8,128)(2,1)S(1)}, bf16[64,8,4096]{2,1,0:T(8,128)(2,1)}, u32[]{:S(2)}) copy-start(bf16[64,8,4096]{2,1,0:T(8,128)(2,1)} %all_to_all.24) | copy-start | bytes 12582916
  159.7 57.0 %all-to-all-start.1 = ((bf16[64,8,2048]{2,1,0:T(8,128)(2,1)}), bf16[64,8,2048]{2,1,0:T(8,128)(2,1)S(1)}, u32[]{:S(2)}, u32[]{:S(2)}) async-start(bf16[64,8,2048]{2,1,0:T(8,128)(2,1)} %fusion.7), calls=%async_computation.2 | async-start | bytes 4194304 | tf_op jit(solution)/shard_map/all_to_all | solution.py:74
Sparse Core Ops, SparseCore 0:
  10.7 98.0 all-gather.1
  151.0 87.9 reduce-scatter.1

commit v5 on v4

--- a/solution.py
+++ b/solution.py
@@ -74,19 +74,13 @@
     returned = lax.all_to_all(row_grad, "exp", split_axis=0, concat_axis=0, tiled=True)
     picked = returned[slot_index].reshape(tok_count, route_count, model_width)
     grad_in = jnp.sum(picked.astype(jnp.float32), axis=1).astype(jnp.bfloat16)
-    summed = lax.psum_scatter(
-        jnp.stack(
-            [
-                contract_rows(x_recv, d_gate),
-                contract_rows(x_recv, d_up),
-                contract_rows(g_recv, hidden),
-            ],
-            axis=0,
-        ).astype(jnp.bfloat16),
-        "rep",
-        scatter_dimension=1,
-        tiled=True,
-    )
+    stacked = lax.dot_general(
+        jnp.stack([x_recv, x_recv, g_recv], axis=0),
+        jnp.stack([d_gate, d_up, hidden], axis=0),
+        (((1,), (1,)), ((0,), (0,))),
+        preferred_element_type=jnp.float32,
+    ).astype(jnp.bfloat16)
+    summed = lax.psum_scatter(stacked, "rep", scatter_dimension=1, tiled=True)
     summed = summed.astype(jnp.float32)
     grad_gate = summed[0]
     grad_up = summed[1]

time: 250 us -> 260 us (1.040)
  local copies, waits for them, and re-layouts: 12.6 us -> 22.5 us
  matrix products: 26.7 us -> 31.5 us
  other arithmetic: 13.1 us -> 8.5 us
    unnamed x11 -> x20, local copies, waits for them, and re-layouts: 0.13 us -> 9.89 us
    dot_general x3 -> x1, matrix products: 5.62 us -> 10.2 us  [per_device(): lax.dot_general(jnp.stack([x_recv, x_recv, g_recv], axis=0), jnp.stack([d...]
    another operation x3 -> x2, other arithmetic: 5.15 us -> 0.65 us  [the longest x1 4.5 us: per_device(): jnp.stack([contract_rows(x_recv, d_gate), contract_rows(x_recv, d_up), co...]
  transfers between devices with their start and end apart: 3 -> 3, of which waited for: 2 -> 2; matrix products, arithmetic and copies ran while one was open for 9% -> 12% of each run, Pallas kernels for 0% -> 0%
where the time goes in v5:
time: 260 us
  blocking collectives  109 us (42%)
  waiting for transfers between devices  67.8 us (26%)
  matrix products  31.5 us (12%)
  local copies, waits for them, and re-layouts  22.5 us (9%)
  between operations  14.3 us (6%)
  other arithmetic  8.5 us (3%)
  starting transfers between devices  5.89 us (2%)
    all_to_all x1, blocking collectives, per_device(): lax.all_to_all(table[by_choice], 'exp', split_axis=0, concat_axis=0, tile...  109 us
    all_to_all x1, waiting for transfers between devices, per_device(): lax.all_to_all(row_grad, 'exp', split_axis=0, concat_axis=0, tiled=True)  51.2 us
    reduce_scatter x1, waiting for transfers between devices, per_device(): summed = lax.psum_scatter(stacked, 'rep', scatter_dimension=1, tiled=True)  16.5 us
    dot_general x1, matrix products, per_device(): lax.dot_general(jnp.stack([x_recv, x_recv, g_recv], axis=0), jnp.stack([d...  10.2 us
    unnamed x20, local copies, waits for them, and re-layouts  9.89 us
    dot_general x2, matrix products, against_cols(): lax.dot_general(left, right, (((1,), (1,)), ((), ())), preferred_element_...  8.82 us
    all_to_all x1, starting transfers between devices, per_device(): lax.all_to_all(row_grad, 'exp', split_axis=0, concat_axis=0, tiled=True)  5.81 us
  transfers between devices with their start and end apart: 3, of which 2 were waited for; matrix products, arithmetic and copies ran while one was open for 12% of the time, Pallas kernels for 0%

profile of v5, /device:TPU:1, one launch (start us, length us, event | category | flops | bytes accessed | tf_op | source)
XLA Modules:
  0.0 259.7 jit_solution(9884113673967928660)
XLA Ops:
  7.2 0.0 all-gather.2.cloned.1.call-start
  7.2 3.3 %pad_maximum_fusion = bf16[3,512,768]{2,1,0:T(8,128)(2,1)} fusion(bf16[1,512,768]{2,1,0:T(8,128)(2,1)} %param.13, bf16[1,512,768]{2,1,0:T(8,128)(2,1)} %param.12, bf16[1,512,768]{2,1,0:T(8,128)(2,1)} %param.11), kind=kLoop, calls=%fused_computation.19 | loop fusion | flops 2359296 | bytes 4718592 | tf_op jit(solution)/shard_map/stack | solution.py:60
  10.5 0.0 copy-start.6
  10.5 0.0 copy-start.7
  10.5 0.0 copy-start.4
  10.5 0.0 copy-start.5
  10.5 0.0 all-gather.2.cloned.1.call-update
  10.5 0.0 reduce-scatter.2.cloned.1.call-start
  10.6 0.6 copy-done.6
  11.1 0.1 copy.13
  11.3 0.1 eq.31
  11.4 0.1 eq.27
  11.6 0.6 reduce-window.6
  12.2 0.2 slice_reduce_fusion
  12.4 0.1 copy.12
  12.5 0.1 mul.74
  12.7 0.1 fusion.24
  12.8 1.4 scatter_custom_fusion
  14.2 0.0 copy-done.7
  14.3 0.0 copy-done.4
  14.3 0.2 fusion.20
  14.5 0.0 copy-done.5
  14.5 0.6 maximum_maximum_fusion
  15.1 4.5 %gather_fusion = bf16[512,4096]{1,0:T(8,128)(2,1)} fusion(bf16[257,4096]{1,0:T(8,128)(2,1)S(1)} %maximum_maximum_fusion, s32[1024]{0:T(1024)S(1)} %pad_clamp_fusion.1), kind=kCustom, calls=%fused_computation | custom fusion | bytes 8390656 | tf_op jit(solution)/shard_map/gather | solution.py:56
  19.6 109.3 %all_to_all.24 = bf16[64,8,4096]{2,1,0:T(8,128)(2,1)S(1)} all-to-all(bf16[64,8,4096]{2,1,0:T(8,128)(2,1)} %bitcast.51), channel_id=1, replica_groups=mesh['rep'=4,'exp'=64] {'exp'}, dimensions={0} | all-to-all | bytes 8388608 | tf_op jit(solution)/shard_map/all_to_all | solution.py:56
  128.9 2.1 fusion.37
  130.9 0.6 copy-done
  131.6 3.9 %copy.18 = bf16[512,2048]{0,1:T(8,128)(2,1)} copy(bf16[512,2048]{1,0:T(8,128)(2,1)} %get-tuple-element.4) | data formatting | bytes 4194304
  135.5 2.6 copy.19
  138.0 4.5 %fusion.10 = f32[512,768]{1,0:T(8,128)S(1)} fusion(bf16[3,2048,768]{2,1,0:T(8,128)(2,1)} %all-gather.2.cloned.1.call-done, bf16[512,4096]{1,0:T(8,128)(2,1)} %bitcast.53), kind=kOutput, calls=%fused_computation.15 | convolution fusion | flops 1610612736 | bytes 6815744 | tf_op jit(solution)/shard_map/dot_general | solution.py:64
  142.5 0.0 copy-done.1
  142.5 3.7 %fusion.9 = f32[512,768]{1,0:T(8,128)S(1)} fusion(bf16[3,2048,768]{2,1,0:T(8,128)(2,1)} %all-gather.2.cloned.1.call-done, bf16[512,4096]{1,0:T(8,128)(2,1)S(1)} %bitcast.54), kind=kOutput, calls=%fused_computation.14 | convolution fusion | flops 1610612736 | bytes 6815744 | tf_op jit(solution)/shard_map/dot_general | solution.py:65
  146.2 0.0 copy-start.2
  146.2 0.0 copy-start.3
  146.2 4.4 %multiply_convert_fusion.2 = (bf16[512,768]{1,0:T(8,128)(2,1)S(1)}, bf16[1,512,768]{2,1,0:T(8,128)(2,1)S(1)}, bf16[512,768]{1,0:T(8,128)(2,1)S(1)}) fusion(f32[512,768]{1,0:T(8,128)S(1)} %fusion.9, f32[512,768]{1,0:T(8,128)S(1)} %fusion.10, bf16[3,2048,768]{2,1,0:T(8,128)(2,1)} %all-gather.2.cloned.1.call-done, bf16[512,4096]{1,0:T(8,128)(2,1)S(1)} %bitcast.55), kind=kOutput, calls=%fused_computation.28 | convolution fusion | flops 1616510976 | bytes 10747904 | tf_op jit(solution)/shard_map/dot_general | solution.py:63
  150.6 0.0 copy-done.2
  150.6 0.0 copy-done.3
  150.6 10.2 %fusion.6 = bf16[3,2048,768]{2,1,0:T(8,128)(2,1)} fusion(bf16[1,512,2048]{1,2,0:T(8,128)(2,1)S(1)} %bitcast.57, bf16[1,512,2048]{1,2,0:T(8,128)(2,1)S(1)} %bitcast.56, bf16[1,512,768]{2,1,0:T(8,128)(2,1)S(1)} %get-tuple-element.7, bf16[1,512,768]{2,1,0:T(8,128)(2,1)S(1)} %bitcast.61, bf16[1,512,768]{2,1,0:T(8,128)(2,1)S(1)} %bitcast.62), kind=kOutput, calls=%fused_computation.9 | convolution fusion | flops 4845207552 | bytes 15990784 | tf_op jit(solution)/shard_map/dot_general | solution.py:77
  160.8 0.0 reduce-scatter.2.cloned.1.call-update
  160.8 3.7 %fusion.11 = f32[512,2048]{1,0:T(8,128)S(1)} fusion(bf16[512,768]{1,0:T(8,128)(2,1)S(1)} %get-tuple-element.6, bf16[3,2048,768]{2,1,0:T(8,128)(2,1)} %all-gather.2.cloned.1.call-done), kind=kOutput, calls=%fused_computation.16 | convolution fusion | flops 1610612736 | bytes 8126464 | tf_op jit(solution)/shard_map/dot_general | solution.py:14
  164.5 5.1 %fusion.13 = bf16[64,8,2048]{2,1,0:T(8,128)(2,1)} fusion(f32[512,2048]{1,0:T(8,128)S(1)} %fusion.11, bf16[512,768]{1,0:T(8,128)(2,1)S(1)} %get-tuple-element.8, bf16[3,2048,768]{2,1,0:T(8,128)(2,1)} %all-gather.2.cloned.1.call-done), kind=kOutput, calls=%fused_computation.18 | convolution fusion | flops 1612709888 | bytes 10223616 | tf_op jit(solution)/shard_map/dot_general | solution.py:14
  169.7 5.8 %all-to-all-start.1 = ((bf16[64,8,2048]{2,1,0:T(8,128)(2,1)}), bf16[64,8,2048]{2,1,0:T(8,128)(2,1)S(1)}, u32[]{:S(2)}, u32[]{:S(2)}) async-start(bf16[64,8,2048]{2,1,0:T(8,128)(2,1)} %fusion.13), calls=%async_computation.2 | async-start | bytes 4194304 | tf_op jit(solution)/shard_map/all_to_all | solution.py:74
  175.5 51.2 %all-to-all-done.1 = bf16[64,8,2048]{2,1,0:T(8,128)(2,1)S(1)} async-done(((bf16[64,8,2048]{2,1,0:T(8,128)(2,1)}), bf16[64,8,2048]{2,1,0:T(8,128)(2,1)S(1)}, u32[]{:S(2)}, u32[]{:S(2)}) %all-to-all-start.1) | async-done | bytes 2097184 | tf_op jit(solution)/shard_map/all_to_all | solution.py:74
  226.7 1.4 gather_fusion.1
  228.0 0.7 reshape.64
  228.8 3.6 %reduce_sum.25 = bf16[128,2048]{1,0:T(8,128)(2,1)} reduce(bf16[128,2,2048]{2,1,0:T(2,128)(2,1)S(1)} %reshape.64, bf16[]{:T(256)} %constant.41.clone.1), dimensions={1}, to_apply=%region_5.6 | reduce | flops 262144 | bytes 1572866 | tf_op jit(solution)/shard_map/reduce_sum | solution.py:76
  232.4 16.5 %reduce-scatter.2.cloned.1.call-done = bf16[3,512,768]{2,1,0:T(8,128)(2,1)} async-done(((bf16[3,2048,768]{2,1,0:T(8,128)(2,1)}), bf16[3,512,768]{2,1,0:T(8,128)(2,1)}) %reduce-scatter.2.cloned.1.call-update) | async-done | bytes 2359312 | tf_op jit(solution)/shard_map/reduce_scatter | solution.py:83
  248.9 3.9 %fusion.38 = (f32[1,512,768]{2,1,0:T(8,128)}, f32[1,512,768]{2,1,0:T(8,128)}, f32[1,512,768]{2,1,0:T(8,128)}) fusion(bf16[3,512,768]{2,1,0:T(8,128)(2,1)} %reduce-scatter.2.cloned.1.call-done), kind=kLoop, calls=%fused_computation.69 | loop fusion | bytes 9437184 | tf_op jit(solution)/shard_map/slice | solution.py:87
  (14 shorter events, 0.1 us)
Async XLA Ops:
  7.2 130.9 %all-gather.2.cloned.1.call-start = ((), (), s32[]{:S(2)}) async-start(), calls=%async_computation.3 | async-start | bytes 11796480 | tf_op jit(solution)/shard_map/all_gather | solution.py:59
  10.5 0.7 copy-start.6
  10.5 3.8 %copy-start.7 = (f32[128,2]{0,1:T(2,128)S(1)}, f32[128,2]{0,1:T(2,128)}, u32[]{:S(2)}) copy-start(f32[128,2]{0,1:T(2,128)} %param.10) | copy-start | bytes 3076
  10.5 3.8 %copy-start.4 = (bf16[128,2048]{1,0:T(8,128)(2,1)S(1)}, bf16[128,2048]{1,0:T(8,128)(2,1)}, u32[]{:S(2)}) copy-start(bf16[128,2048]{1,0:T(8,128)(2,1)} %param.8) | copy-start | bytes 1572868
  10.5 4.0 %copy-start.5 = (bf16[128,2048]{1,0:T(8,128)(2,1)S(1)}, bf16[128,2048]{1,0:T(8,128)(2,1)}, u32[]{:S(2)}) copy-start(bf16[128,2048]{1,0:T(8,128)(2,1)} %param.7) | copy-start | bytes 1572868
  10.5 238.4 %reduce-scatter.2.cloned.1.call-start = ((), (), s32[]{:S(2)}) async-start(), calls=%async_computation.4 | async-start | bytes 11796480 | tf_op jit(solution)/shard_map/reduce_scatter | solution.py:83
  128.9 2.7 %copy-start = (bf16[64,8,4096]{2,1,0:T(8,128)(2,1)}, bf16[64,8,4096]{2,1,0:T(8,128)(2,1)S(1)}, u32[]{:S(2)}) copy-start(bf16[64,8,4096]{2,1,0:T(8,128)(2,1)S(1)} %all_to_all.24) | copy-start | bytes 12582916
  138.0 4.5 %copy-start.1 = (bf16[64,8,4096]{2,1,0:T(8,128)(2,1)S(1)}, bf16[64,8,4096]{2,1,0:T(8,128)(2,1)}, u32[]{:S(2)}) copy-start(bf16[64,8,4096]{2,1,0:T(8,128)(2,1)} %copy-done) | copy-start | bytes 12582916
  146.2 4.4 %copy-start.2 = (bf16[512,2048]{0,1:T(8,128)(2,1)S(1)}, bf16[512,2048]{0,1:T(8,128)(2,1)}, u32[]{:S(2)}) copy-start(bf16[512,2048]{0,1:T(8,128)(2,1)} %copy.18) | copy-start | bytes 6291460
  146.2 4.4 %copy-start.3 = (bf16[512,2048]{0,1:T(8,128)(2,1)S(1)}, bf16[512,2048]{0,1:T(8,128)(2,1)}, u32[]{:S(2)}) copy-start(bf16[512,2048]{0,1:T(8,128)(2,1)} %copy.19) | copy-start | bytes 6291460
  169.7 57.0 %all-to-all-start.1 = ((bf16[64,8,2048]{2,1,0:T(8,128)(2,1)}), bf16[64,8,2048]{2,1,0:T(8,128)(2,1)S(1)}, u32[]{:S(2)}, u32[]{:S(2)}) async-start(bf16[64,8,2048]{2,1,0:T(8,128)(2,1)} %fusion.13), calls=%async_computation.2 | async-start | bytes 4194304 | tf_op jit(solution)/shard_map/all_to_all | solution.py:74
Sparse Core Ops, SparseCore 0:
  10.6 98.0 all-gather.1
  160.9 87.9 reduce-scatter.1

commit v6 on v5

--- a/solution.py
+++ b/solution.py
@@ -74,12 +74,15 @@
     returned = lax.all_to_all(row_grad, "exp", split_axis=0, concat_axis=0, tiled=True)
     picked = returned[slot_index].reshape(tok_count, route_count, model_width)
     grad_in = jnp.sum(picked.astype(jnp.float32), axis=1).astype(jnp.bfloat16)
-    stacked = lax.dot_general(
-        jnp.stack([x_recv, x_recv, g_recv], axis=0),
-        jnp.stack([d_gate, d_up, hidden], axis=0),
-        (((1,), (1,)), ((0,), (0,))),
-        preferred_element_type=jnp.float32,
-    ).astype(jnp.bfloat16)
+    stacked = jnp.zeros((3, model_width, d_gate.shape[1]), jnp.bfloat16)
+    for which, part in enumerate(
+        (
+            contract_rows(x_recv, d_gate),
+            contract_rows(x_recv, d_up),
+            contract_rows(g_recv, hidden),
+        )
+    ):
+        stacked = lax.dynamic_update_slice(stacked, part.astype(jnp.bfloat16)[None], (which, 0, 0))
     summed = lax.psum_scatter(stacked, "rep", scatter_dimension=1, tiled=True)
     summed = summed.astype(jnp.float32)
     grad_gate = summed[0]

time: 260 us -> 254 us (0.977)
  local copies, waits for them, and re-layouts: 22.5 us -> 17.5 us
    unnamed x20 -> x15, local copies, waits for them, and re-layouts: 9.89 us -> 0.73 us
    dynamic_update_slice x0 -> x1, local copies, waits for them, and re-layouts: none -> 4.27 us  [per_device(): lax.dynamic_update_slice(stacked, part.astype(jnp.bfloat16)[None], (which...]
    dot_general x1 -> x3, matrix products: 10.2 us -> 8.96 us  [contract_rows(): lax.dot_general(left, right, (((0,), (0,)), ((), ())), preferred_element_...]
  transfers between devices with their start and end apart: 3 -> 3, of which waited for: 2 -> 2; matrix products, arithmetic and copies ran while one was open for 12% -> 9% of each run, Pallas kernels for 0% -> 0%
where the time goes in v6:
time: 254 us
  blocking collectives  109 us (43%)
  waiting for transfers between devices  67.6 us (27%)
  matrix products  30.7 us (12%)
  local copies, waits for them, and re-layouts  17.5 us (7%)
  between operations  14.3 us (6%)
  other arithmetic  8.52 us (3%)
  starting transfers between devices  5.91 us (2%)
    all_to_all x1, blocking collectives, per_device(): lax.all_to_all(table[by_choice], 'exp', split_axis=0, concat_axis=0, tile...  109 us
    all_to_all x1, waiting for transfers between devices, per_device(): lax.all_to_all(row_grad, 'exp', split_axis=0, concat_axis=0, tiled=True)  51.2 us
    reduce_scatter x1, waiting for transfers between devices, per_device(): summed = lax.psum_scatter(stacked, 'rep', scatter_dimension=1, tiled=True)  16.3 us
    dot_general x2, matrix products, against_cols(): lax.dot_general(left, right, (((1,), (1,)), ((), ())), preferred_element_...  9 us
    dot_general x3, matrix products, contract_rows(): lax.dot_general(left, right, (((0,), (0,)), ((), ())), preferred_element_...  8.96 us
    all_to_all x1, starting transfers between devices, per_device(): lax.all_to_all(row_grad, 'exp', split_axis=0, concat_axis=0, tiled=True)  5.83 us
  transfers between devices with their start and end apart: 3, of which 2 were waited for; matrix products, arithmetic and copies ran while one was open for 9% of the time, Pallas kernels for 0%

profile of v6, /device:TPU:1, one launch (start us, length us, event | category | flops | bytes accessed | tf_op | source)
XLA Modules:
  0.0 253.7 jit_solution(2742793735415992645)
XLA Ops:
  7.2 0.0 all-gather.2.cloned.1.call-start
  7.2 3.3 %pad_maximum_fusion = bf16[3,512,768]{2,1,0:T(8,128)(2,1)} fusion(bf16[1,512,768]{2,1,0:T(8,128)(2,1)} %param.13, bf16[1,512,768]{2,1,0:T(8,128)(2,1)} %param.12, bf16[1,512,768]{2,1,0:T(8,128)(2,1)} %param.11), kind=kLoop, calls=%fused_computation.18 | loop fusion | flops 2359296 | bytes 4718592 | tf_op jit(solution)/shard_map/stack | solution.py:60
  10.5 0.0 copy-start.3
  10.5 0.0 copy-start.4
  10.5 0.0 copy-start.1
  10.5 0.0 copy-start.2
  10.5 0.0 all-gather.2.cloned.1.call-update
  10.5 0.0 reduce-scatter.2.cloned.1.call-start
  10.6 0.6 copy-done.3
  11.2 0.1 copy.12
  11.3 0.1 eq.31
  11.4 0.1 eq.27
  11.6 0.1 copy.11
  11.7 0.1 mul.74
  11.8 0.6 reduce-window.6
  12.4 0.2 slice_reduce_fusion
  12.7 0.1 fusion.17
  12.8 1.4 scatter_custom_fusion
  14.3 0.0 copy-done.4
  14.3 0.0 copy-done.1
  14.3 0.2 fusion.13
  14.5 0.0 copy-done.2
  14.5 0.6 maximum_maximum_fusion
  15.1 4.4 %gather_fusion = bf16[512,4096]{1,0:T(8,128)(2,1)} fusion(bf16[257,4096]{1,0:T(8,128)(2,1)S(1)} %maximum_maximum_fusion, s32[1024]{0:T(1024)S(1)} %pad_clamp_fusion.1), kind=kCustom, calls=%fused_computation | custom fusion | bytes 8390656 | tf_op jit(solution)/shard_map/gather | solution.py:56
  19.5 109.4 %all_to_all.24 = bf16[64,8,4096]{2,1,0:T(8,128)(2,1)} all-to-all(bf16[64,8,4096]{2,1,0:T(8,128)(2,1)} %bitcast.54), channel_id=1, replica_groups=mesh['rep'=4,'exp'=64] {'exp'}, dimensions={0} | all-to-all | bytes 8388608 | tf_op jit(solution)/shard_map/all_to_all | solution.py:56
  128.9 0.0 all-gather.2.cloned.1.call-done
  128.9 0.0 copy-start
  128.9 4.5 %fusion.4 = f32[512,768]{1,0:T(8,128)S(1)} fusion(bf16[3,2048,768]{2,1,0:T(8,128)(2,1)} %all-gather.2.cloned.1.call-done, bf16[512,4096]{1,0:T(8,128)(2,1)} %bitcast.55), kind=kOutput, calls=%fused_computation.16 | convolution fusion | flops 1610612736 | bytes 6815744 | tf_op jit(solution)/shard_map/dot_general | solution.py:63
  133.4 0.0 copy-done
  133.4 3.7 %fusion.2 = f32[512,768]{1,0:T(8,128)S(1)} fusion(bf16[3,2048,768]{2,1,0:T(8,128)(2,1)} %all-gather.2.cloned.1.call-done, bf16[512,4096]{1,0:T(8,128)(2,1)S(1)} %bitcast.56), kind=kOutput, calls=%fused_computation.14 | convolution fusion | flops 1610612736 | bytes 6815744 | tf_op jit(solution)/shard_map/dot_general | solution.py:64
  137.0 0.0 copy-start.5
  137.1 4.6 %multiply_convert_fusion.1 = (bf16[512,768]{1,0:T(8,128)(2,1)S(1)}, bf16[512,768]{1,0:T(8,128)(2,1)S(1)}) fusion(f32[512,768]{1,0:T(8,128)S(1)} %fusion.4, f32[512,768]{1,0:T(8,128)S(1)} %fusion.2, bf16[3,2048,768]{2,1,0:T(8,128)(2,1)} %all-gather.2.cloned.1.call-done, bf16[512,4096]{1,0:T(8,128)(2,1)S(1)} %bitcast.57), kind=kOutput, calls=%fused_computation.23 | convolution fusion | flops 1615724544 | bytes 9961472 | tf_op jit(solution)/shard_map/dot_general | solution.py:65
  141.6 0.0 copy-done.5
  141.6 1.8 fusion.1
  143.5 4.3 %dynamic_update_slice.9 = bf16[3,2048,768]{2,1,0:T(8,128)(2,1)} pad(bf16[1,2048,768]{2,1,0:T(8,128)(2,1)S(1)} %fusion.1, bf16[]{:T(256)} %constant.25.clone.1), padding=0_2x0_0x0_0 | pad | bytes 12582914 | tf_op jit(solution)/shard_map/dynamic_update_slice | solution.py:85
  147.8 3.5 %bitcast_dynamic-update-slice_fusion.1 = bf16[3,2048,768]{2,1,0:T(8,128)(2,1)} fusion(bf16[3,2048,768]{2,1,0:T(8,128)(2,1)} %dynamic_update_slice.9, bf16[512,768]{1,0:T(8,128)(2,1)S(1)} %get-tuple-element.4, bf16[512,4096]{1,0:T(8,128)(2,1)S(1)} %bitcast.59), kind=kOutput, calls=%fused_computation.12 | convolution fusion | flops 1612185600 | bytes 6029312 | tf_op jit(solution)/shard_map/dot_general | solution.py:8
  151.3 0.0 copy-done.6
  151.3 3.6 %bitcast_dynamic-update-slice_fusion = bf16[3,2048,768]{2,1,0:T(8,128)(2,1)} fusion(bf16[3,2048,768]{2,1,0:T(8,128)(2,1)} %bitcast_dynamic-update-slice_fusion.1, bf16[512,4096]{1,0:T(8,128)(2,1)S(1)} %bitcast.60, f32[512,768]{1,0:T(8,128)S(1)} %copy-done.6, f32[512,768]{1,0:T(8,128)S(1)} %fusion.4), kind=kOutput, calls=%fused_computation.11 | convolution fusion | flops 1614544896 | bytes 8388608 | tf_op jit(solution)/shard_map/dot_general | solution.py:8
  154.9 0.0 reduce-scatter.2.cloned.1.call-update
  154.9 3.9 %fusion.3 = f32[512,2048]{1,0:T(8,128)S(1)} fusion(bf16[512,768]{1,0:T(8,128)(2,1)S(1)} %get-tuple-element.5, bf16[3,2048,768]{2,1,0:T(8,128)(2,1)} %all-gather.2.cloned.1.call-done), kind=kOutput, calls=%fused_computation.15 | convolution fusion | flops 1610612736 | bytes 8126464 | tf_op jit(solution)/shard_map/dot_general | solution.py:14
  158.8 5.1 %fusion.5 = bf16[64,8,2048]{2,1,0:T(8,128)(2,1)} fusion(f32[512,2048]{1,0:T(8,128)S(1)} %fusion.3, bf16[512,768]{1,0:T(8,128)(2,1)S(1)} %get-tuple-element.4, bf16[3,2048,768]{2,1,0:T(8,128)(2,1)} %all-gather.2.cloned.1.call-done), kind=kOutput, calls=%fused_computation.17 | convolution fusion | flops 1612709888 | bytes 10223616 | tf_op jit(solution)/shard_map/dot_general | solution.py:14
  163.9 5.8 %all-to-all-start.1 = ((bf16[64,8,2048]{2,1,0:T(8,128)(2,1)}), bf16[64,8,2048]{2,1,0:T(8,128)(2,1)S(1)}, u32[]{:S(2)}, u32[]{:S(2)}) async-start(bf16[64,8,2048]{2,1,0:T(8,128)(2,1)} %fusion.5), calls=%async_computation.2 | async-start | bytes 4194304 | tf_op jit(solution)/shard_map/all_to_all | solution.py:74
  169.8 51.2 %all-to-all-done.1 = bf16[64,8,2048]{2,1,0:T(8,128)(2,1)S(1)} async-done(((bf16[64,8,2048]{2,1,0:T(8,128)(2,1)}), bf16[64,8,2048]{2,1,0:T(8,128)(2,1)S(1)}, u32[]{:S(2)}, u32[]{:S(2)}) %all-to-all-start.1) | async-done | bytes 2097184 | tf_op jit(solution)/shard_map/all_to_all | solution.py:74
  221.0 1.4 gather_fusion.1
  222.3 0.7 reshape.64
  223.0 3.6 %reduce_sum.25 = bf16[128,2048]{1,0:T(8,128)(2,1)} reduce(bf16[128,2,2048]{2,1,0:T(2,128)(2,1)S(1)} %reshape.64, bf16[]{:T(256)} %constant.25.clone.1), dimensions={1}, to_apply=%region_5.6 | reduce | flops 262144 | bytes 1572866 | tf_op jit(solution)/shard_map/reduce_sum | solution.py:76
  226.7 16.3 %reduce-scatter.2.cloned.1.call-done = bf16[3,512,768]{2,1,0:T(8,128)(2,1)} async-done(((bf16[3,2048,768]{2,1,0:T(8,128)(2,1)}), bf16[3,512,768]{2,1,0:T(8,128)(2,1)}) %reduce-scatter.2.cloned.1.call-update) | async-done | bytes 2359312 | tf_op jit(solution)/shard_map/reduce_scatter | solution.py:86
  243.0 3.9 %fusion.27 = (f32[1,512,768]{2,1,0:T(8,128)}, f32[1,512,768]{2,1,0:T(8,128)}, f32[1,512,768]{2,1,0:T(8,128)}) fusion(bf16[3,512,768]{2,1,0:T(8,128)(2,1)} %reduce-scatter.2.cloned.1.call-done), kind=kLoop, calls=%fused_computation.64 | loop fusion | bytes 9437184 | tf_op jit(solution)/shard_map/slice | solution.py:90
  (12 shorter events, 0.1 us)
Async XLA Ops:
  7.2 121.7 %all-gather.2.cloned.1.call-start = ((), (), s32[]{:S(2)}) async-start(), calls=%async_computation.3 | async-start | bytes 11796480 | tf_op jit(solution)/shard_map/all_gather | solution.py:59
  10.5 0.7 copy-start.3
  10.5 3.8 %copy-start.4 = (f32[128,2]{0,1:T(2,128)S(1)}, f32[128,2]{0,1:T(2,128)}, u32[]{:S(2)}) copy-start(f32[128,2]{0,1:T(2,128)} %param.10) | copy-start | bytes 3076
  10.5 3.8 %copy-start.1 = (bf16[128,2048]{1,0:T(8,128)(2,1)S(1)}, bf16[128,2048]{1,0:T(8,128)(2,1)}, u32[]{:S(2)}) copy-start(bf16[128,2048]{1,0:T(8,128)(2,1)} %param.8) | copy-start | bytes 1572868
  10.5 4.0 %copy-start.2 = (bf16[128,2048]{1,0:T(8,128)(2,1)S(1)}, bf16[128,2048]{1,0:T(8,128)(2,1)}, u32[]{:S(2)}) copy-start(bf16[128,2048]{1,0:T(8,128)(2,1)} %param.7) | copy-start | bytes 1572868
  10.5 232.5 %reduce-scatter.2.cloned.1.call-start = ((), (), s32[]{:S(2)}) async-start(), calls=%async_computation.4 | async-start | bytes 11796480 | tf_op jit(solution)/shard_map/reduce_scatter | solution.py:86
  128.9 4.5 %copy-start = (bf16[64,8,4096]{2,1,0:T(8,128)(2,1)S(1)}, bf16[64,8,4096]{2,1,0:T(8,128)(2,1)}, u32[]{:S(2)}) copy-start(bf16[64,8,4096]{2,1,0:T(8,128)(2,1)} %all_to_all.24) | copy-start | bytes 12582916
  137.0 4.6 %copy-start.5 = (f32[512,768]{1,0:T(8,128)}, f32[512,768]{1,0:T(8,128)S(1)}, u32[]{:S(2)}) copy-start(f32[512,768]{1,0:T(8,128)S(1)} %fusion.2) | copy-start | bytes 4718596
  147.7 3.5 %copy-start.6 = (f32[512,768]{1,0:T(8,128)S(1)}, f32[512,768]{1,0:T(8,128)}, u32[]{:S(2)}) copy-start(f32[512,768]{1,0:T(8,128)} %copy-done.5) | copy-start | bytes 4718596
  163.9 57.0 %all-to-all-start.1 = ((bf16[64,8,2048]{2,1,0:T(8,128)(2,1)}), bf16[64,8,2048]{2,1,0:T(8,128)(2,1)S(1)}, u32[]{:S(2)}, u32[]{:S(2)}) async-start(bf16[64,8,2048]{2,1,0:T(8,128)(2,1)} %fusion.5), calls=%async_computation.2 | async-start | bytes 4194304 | tf_op jit(solution)/shard_map/all_to_all | solution.py:74
Sparse Core Ops, SparseCore 0:
  10.6 98.0 all-gather.1
  155.0 87.9 reduce-scatter.1

commit v7 on v4

--- a/solution.py
+++ b/solution.py
@@ -29,11 +29,10 @@
     )
     slot_rank = jnp.sum((jnp.cumsum(onehot, axis=0) - 1) * onehot, axis=1)
     slot_index = flat_routes * slot_cap + slot_rank
-    source = (
-        jnp.full((slot_total,), route_total, jnp.int32)
-        .at[slot_index]
-        .set(jnp.arange(route_total, dtype=jnp.int32))
-    )
+    match = slot_index[None, :] == jnp.arange(slot_total, dtype=jnp.int32)[:, None]
+    source = jnp.sum(
+        jnp.where(match, jnp.arange(route_total, dtype=jnp.int32)[None, :], 0), axis=1
+    ) + jnp.where(jnp.any(match, axis=1), 0, route_total)
     table = jnp.concatenate(
         [
             jnp.concatenate(
@@ -56,10 +55,9 @@
     both_recv = lax.all_to_all(table[by_choice], "exp", split_axis=0, concat_axis=0, tiled=True)
     x_recv = both_recv[:, :model_width]
     g_recv = both_recv[:, model_width:]
-    full_all = lax.all_gather(
-        jnp.stack([w_gate[0], w_up[0], w_down[0]], axis=0), "rep", axis=1, tiled=True
-    )
-    full_gate, full_up, full_down = full_all[0], full_all[1], full_all[2]
+    gate_up = lax.all_gather(jnp.stack([w_gate[0], w_up[0]], axis=0), "rep", axis=1, tiled=True)
+    full_gate, full_up = gate_up[0], gate_up[1]
+    full_down = lax.all_gather(w_down[0], "rep", axis=0, tiled=True)
     pre_gate = jnp.dot(x_recv, full_gate, preferred_element_type=jnp.float32)
     pre_up = jnp.dot(x_recv, full_up, preferred_element_type=jnp.float32)
     hid_grad = jnp.dot(g_recv, full_down, preferred_element_type=jnp.float32)

time: 250 us -> 254 us (1.016)
  blocking collectives: 109 us -> 0 us
  waiting for transfers between devices: 67.8 us -> 164 us
  starting transfers between devices: 5.91 us -> 19.4 us
  matrix products: 26.7 us -> 32 us
    all_to_all x1 -> x0, blocking collectives: 109 us -> none  [per_device(): lax.all_to_all(table[by_choice], 'exp', split_axis=0, concat_axis=0, tile...]
    all_to_all x0 -> x1, waiting for transfers between devices: none -> 71.5 us  [per_device(): lax.all_to_all(table[by_choice], 'exp', split_axis=0, concat_axis=0, tile...]
    all_gather x1 -> x2, waiting for transfers between devices: 0.01 us -> 24.2 us  [the longest x1 24.1 us: per_device(): full_down = lax.all_gather(w_down[0], 'rep', axis=0, tiled=True)]
    all_to_all x0 -> x1, starting transfers between devices: none -> 13.3 us  [per_device(): lax.all_to_all(table[by_choice], 'exp', split_axis=0, concat_axis=0, tile...]
    dot_general x3, matrix products: 5.62 us -> 10.4 us  [contract_rows(): lax.dot_general(left, right, (((0,), (0,)), ((), ())), preferred_element_...]
  transfers between devices with their start and end apart: 3 -> 5, of which waited for: 2 -> 4; matrix products, arithmetic and copies ran while one was open for 9% -> 11% of each run, Pallas kernels for 0% -> 0%
where the time goes in v7:
time: 254 us
  waiting for transfers between devices  164 us (65%)
  matrix products  32 us (13%)
  starting transfers between devices  19.4 us (8%)
  between operations  14 us (6%)
  other arithmetic  13.2 us (5%)
  local copies, waits for them, and re-layouts  11.2 us (4%)
    all_to_all x1, waiting for transfers between devices, per_device(): lax.all_to_all(table[by_choice], 'exp', split_axis=0, concat_axis=0, tile...  71.5 us
    all_to_all x1, waiting for transfers between devices, per_device(): lax.all_to_all(row_grad, 'exp', split_axis=0, concat_axis=0, tiled=True)  50.9 us
    all_gather x1, waiting for transfers between devices, per_device(): full_down = lax.all_gather(w_down[0], 'rep', axis=0, tiled=True)  24.1 us
    reduce_scatter x1, waiting for transfers between devices, per_device(): lax.psum_scatter(jnp.stack([contract_rows(x_recv, d_gate), contract_rows(...  16.4 us
    all_to_all x1, starting transfers between devices, per_device(): lax.all_to_all(table[by_choice], 'exp', split_axis=0, concat_axis=0, tile...  13.3 us
    dot_general x3, matrix products, contract_rows(): lax.dot_general(left, right, (((0,), (0,)), ((), ())), preferred_element_...  10.4 us
    dot_general x2, matrix products, against_cols(): lax.dot_general(left, right, (((1,), (1,)), ((), ())), preferred_element_...  8.85 us
    all_to_all x1, starting transfers between devices, per_device(): lax.all_to_all(row_grad, 'exp', split_axis=0, concat_axis=0, tiled=True)  5.8 us
  transfers between devices with their start and end apart: 5, of which 4 were waited for; matrix products, arithmetic and copies ran while one was open for 11% of the time, Pallas kernels for 0%

profile of v7, /device:TPU:1, one launch (start us, length us, event | category | flops | bytes accessed | tf_op | source)
XLA Modules:
  0.0 253.6 jit_solution(8295068193983868265)
XLA Ops:
  7.2 0.0 copy-start.2
  7.2 0.0 copy-start.3
  7.2 0.0 copy-start
  7.2 0.0 all-gather.6.cloned.1.call-start
  7.2 0.7 all-gather.6.cloned.1.call-update
  7.9 0.0 copy-start.1
  7.9 0.0 all-gather.4.cloned.1.call-start
  8.0 2.7 %pad_maximum_fusion.1 = bf16[2,512,768]{2,1,0:T(8,128)(2,1)} fusion(bf16[1,512,768]{2,1,0:T(8,128)(2,1)} %param.12, bf16[1,512,768]{2,1,0:T(8,128)(2,1)} %param.11), kind=kLoop, calls=%fused_computation.21 | loop fusion | flops 786432 | bytes 3145728 | tf_op jit(solution)/shard_map/stack | solution.py:58
  10.7 0.0 all-gather.4.cloned.1.call-update
  10.7 0.0 copy-done.2
  10.7 0.1 copy.15
  10.8 0.1 eq.41
  11.0 0.1 reshape.176
  11.1 0.6 reduce-window.6
  11.8 0.2 slice_reduce_fusion
  12.0 0.1 fusion.21
  12.1 0.2 select_reduce_fusion
  12.3 0.2 fusion.18
  12.5 0.0 copy-done.3
  12.5 0.2 fusion.16
  12.8 0.0 copy-done.1
  12.8 0.6 maximum_maximum_fusion
  13.4 4.4 %gather_fusion = bf16[512,4096]{1,0:T(8,128)(2,1)} fusion(bf16[257,4096]{1,0:T(8,128)(2,1)S(1)} %maximum_maximum_fusion, s32[1024]{0:T(1024)S(1)} %pad_clamp_fusion.1), kind=kCustom, calls=%fused_computation | custom fusion | bytes 8390656 | tf_op jit(solution)/shard_map/gather | solution.py:55
  17.8 13.3 %all-to-all-start = ((bf16[64,8,4096]{2,1,0:T(8,128)(2,1)}), bf16[64,8,4096]{2,1,0:T(8,128)(2,1)}, u32[]{:S(2)}, u32[]{:S(2)}) async-start(bf16[64,8,4096]{2,1,0:T(8,128)(2,1)} %bitcast.55), calls=%async_computation | async-start | bytes 8388608 | tf_op jit(solution)/shard_map/all_to_all | solution.py:55
  31.1 0.2 reduce-scatter.2.cloned.1.call-start
  31.4 24.1 %all-gather.6.cloned.1.call-done = bf16[1,2048,768]{2,1,0:T(8,128)(2,1)} async-done(((bf16[1,512,768]{2,1,0:T(8,128)(2,1)}), bf16[1,2048,768]{2,1,0:T(8,128)(2,1)}) %all-gather.6.cloned.1.call-update) | async-done | bytes 3145744 | tf_op jit(solution)/shard_map/all_gather | solution.py:60
  55.5 71.5 %all-to-all-done = bf16[64,8,4096]{2,1,0:T(8,128)(2,1)} async-done(((bf16[64,8,4096]{2,1,0:T(8,128)(2,1)}), bf16[64,8,4096]{2,1,0:T(8,128)(2,1)}, u32[]{:S(2)}, u32[]{:S(2)}) %all-to-all-start) | async-done | bytes 4194336 | tf_op jit(solution)/shard_map/all_to_all | solution.py:55
  127.0 4.3 %fusion = f32[512,768]{1,0:T(8,128)S(1)} fusion(bf16[1,2048,768]{2,1,0:T(8,128)(2,1)} %all-gather.6.cloned.1.call-done, bf16[512,4096]{1,0:T(8,128)(2,1)} %bitcast.6), kind=kOutput, calls=%fused_computation.9 | convolution fusion | flops 1610612736 | bytes 6815744 | tf_op jit(solution)/shard_map/dot_general | solution.py:63
  131.3 0.0 all-gather.4.cloned.1.call-done
  131.3 4.5 %fusion.5 = f32[512,768]{1,0:T(8,128)S(1)} fusion(bf16[2,2048,768]{2,1,0:T(8,128)(2,1)} %all-gather.4.cloned.1.call-done, bf16[512,4096]{1,0:T(8,128)(2,1)} %bitcast.6), kind=kOutput, calls=%fused_computation.14 | convolution fusion | flops 1610612736 | bytes 6815744 | tf_op jit(solution)/shard_map/dot_general | solution.py:62
  135.8 0.0 copy-done.4
  135.8 3.9 %multiply_convert_fusion.2 = (bf16[512,768]{1,0:T(8,128)(2,1)S(1)}, bf16[512,768]{1,0:T(8,128)(2,1)S(1)}, f32[512,768]{1,0:T(8,128)S(1)}) fusion(f32[512,768]{1,0:T(8,128)S(1)} %fusion, f32[512,768]{1,0:T(8,128)S(1)} %fusion.5, bf16[2,2048,768]{2,1,0:T(8,128)(2,1)S(1)} %copy-done.4, bf16[512,4096]{1,0:T(8,128)(2,1)} %bitcast.6), kind=kOutput, calls=%fused_computation.24 | convolution fusion | flops 1615724544 | bytes 11534336 | tf_op jit(solution)/shard_map/dot_general | solution.py:61
  139.7 3.4 %fusion.2 = bf16[1,2048,768]{2,1,0:T(8,128)(2,1)S(1)} fusion(bf16[512,768]{1,0:T(8,128)(2,1)S(1)} %get-tuple-element.4, bf16[512,4096]{1,0:T(8,128)(2,1)} %bitcast.6), kind=kOutput, calls=%fused_computation.11 | convolution fusion | flops 1612185600 | bytes 6029312 | tf_op jit(solution)/shard_map/dot_general | solution.py:8
  143.2 3.4 %fusion.3 = bf16[1,2048,768]{2,1,0:T(8,128)(2,1)S(1)} fusion(bf16[512,768]{1,0:T(8,128)(2,1)S(1)} %get-tuple-element.5, bf16[512,4096]{1,0:T(8,128)(2,1)} %bitcast.6), kind=kOutput, calls=%fused_computation.12 | convolution fusion | flops 1612185600 | bytes 6029312 | tf_op jit(solution)/shard_map/dot_general | solution.py:8
  146.6 3.6 %fusion.4 = bf16[1,2048,768]{2,1,0:T(8,128)(2,1)S(1)} fusion(bf16[512,4096]{1,0:T(8,128)(2,1)} %bitcast.6, f32[512,768]{1,0:T(8,128)S(1)} %fusion.5, f32[512,768]{1,0:T(8,128)S(1)} %get-tuple-element.13), kind=kOutput, calls=%fused_computation.13 | convolution fusion | flops 1614544896 | bytes 8388608 | tf_op jit(solution)/shard_map/dot_general | solution.py:8
  150.2 4.8 %pad_maximum_fusion = bf16[3,2048,768]{2,1,0:T(8,128)(2,1)} fusion(bf16[1,2048,768]{2,1,0:T(8,128)(2,1)S(1)} %fusion.4, bf16[1,2048,768]{2,1,0:T(8,128)(2,1)S(1)} %fusion.3, bf16[1,2048,768]{2,1,0:T(8,128)(2,1)S(1)} %fusion.2), kind=kLoop, calls=%fused_computation.2 | loop fusion | flops 9437184 | bytes 18874368 | tf_op jit(solution)/shard_map/stack | solution.py:76
  155.0 0.0 reduce-scatter.2.cloned.1.call-update
  155.1 3.7 %fusion.6 = f32[512,2048]{1,0:T(8,128)S(1)} fusion(bf16[512,768]{1,0:T(8,128)(2,1)S(1)} %get-tuple-element.4, bf16[2,2048,768]{2,1,0:T(8,128)(2,1)} %all-gather.4.cloned.1.call-done), kind=kOutput, calls=%fused_computation.15 | convolution fusion | flops 1610612736 | bytes 8126464 | tf_op jit(solution)/shard_map/dot_general | solution.py:14
  158.8 5.1 %fusion.8 = bf16[64,8,2048]{2,1,0:T(8,128)(2,1)} fusion(f32[512,2048]{1,0:T(8,128)S(1)} %fusion.6, bf16[512,768]{1,0:T(8,128)(2,1)S(1)} %get-tuple-element.5, bf16[2,2048,768]{2,1,0:T(8,128)(2,1)} %all-gather.4.cloned.1.call-done), kind=kOutput, calls=%fused_computation.17 | convolution fusion | flops 1612709888 | bytes 10223616 | tf_op jit(solution)/shard_map/dot_general | solution.py:14
  163.9 5.8 %all-to-all-start.1 = ((bf16[64,8,2048]{2,1,0:T(8,128)(2,1)}), bf16[64,8,2048]{2,1,0:T(8,128)(2,1)S(1)}, u32[]{:S(2)}, u32[]{:S(2)}) async-start(bf16[64,8,2048]{2,1,0:T(8,128)(2,1)} %fusion.8), calls=%async_computation.2 | async-start | bytes 4194304 | tf_op jit(solution)/shard_map/all_to_all | solution.py:72
  169.7 0.1 copy.18
  169.9 0.1 mul.101
  170.0 50.9 %all-to-all-done.1 = bf16[64,8,2048]{2,1,0:T(8,128)(2,1)S(1)} async-done(((bf16[64,8,2048]{2,1,0:T(8,128)(2,1)}), bf16[64,8,2048]{2,1,0:T(8,128)(2,1)S(1)}, u32[]{:S(2)}, u32[]{:S(2)}) %all-to-all-start.1) | async-done | bytes 2097184 | tf_op jit(solution)/shard_map/all_to_all | solution.py:72
  220.9 1.4 gather_fusion.1
  222.3 0.7 reshape.178
  223.0 3.7 %reduce_sum.35 = bf16[128,2048]{1,0:T(8,128)(2,1)} reduce(bf16[128,2,2048]{2,1,0:T(2,128)(2,1)S(1)} %reshape.178, bf16[]{:T(256)} %constant.42.clone.1), dimensions={1}, to_apply=%region_6.7 | reduce | flops 262144 | bytes 1572866 | tf_op jit(solution)/shard_map/reduce_sum | solution.py:74
  226.7 16.4 %reduce-scatter.2.cloned.1.call-done = bf16[3,512,768]{2,1,0:T(8,128)(2,1)} async-done(((bf16[3,2048,768]{2,1,0:T(8,128)(2,1)}), bf16[3,512,768]{2,1,0:T(8,128)(2,1)}) %reduce-scatter.2.cloned.1.call-update) | async-done | bytes 2359312 | tf_op jit(solution)/shard_map/reduce_scatter | solution.py:75
  243.1 3.9 %fusion.26 = (f32[1,512,768]{2,1,0:T(8,128)}, f32[1,512,768]{2,1,0:T(8,128)}, f32[1,512,768]{2,1,0:T(8,128)}) fusion(bf16[3,512,768]{2,1,0:T(8,128)(2,1)} %reduce-scatter.2.cloned.1.call-done), kind=kLoop, calls=%fused_computation.64 | loop fusion | bytes 9437184 | tf_op jit(solution)/shard_map/slice | solution.py:91
  (14 shorter events, 0.1 us)
Async XLA Ops:
  7.2 3.6 %copy-start.2 = (s32[128,2]{0,1:T(2,128)S(1)}, s32[128,2]{0,1:T(2,128)}, u32[]{:S(2)}) copy-start(s32[128,2]{0,1:T(2,128)} %param.9) | copy-start | bytes 3076
  7.2 5.3 %copy-start.3 = (f32[128,2]{0,1:T(2,128)S(1)}, f32[128,2]{0,1:T(2,128)}, u32[]{:S(2)}) copy-start(f32[128,2]{0,1:T(2,128)} %param.10) | copy-start | bytes 3076
  7.2 5.3 %copy-start = (bf16[128,2048]{1,0:T(8,128)(2,1)S(1)}, bf16[128,2048]{1,0:T(8,128)(2,1)}, u32[]{:S(2)}) copy-start(bf16[128,2048]{1,0:T(8,128)(2,1)} %param.8) | copy-start | bytes 1572868
  7.2 48.3 %all-gather.6.cloned.1.call-start = ((), (), s32[]{:S(2)}) async-start(), calls=%async_computation.5 | async-start | bytes 3932160 | tf_op jit(solution)/shard_map/all_gather | solution.py:60
  7.9 4.8 %copy-start.1 = (bf16[128,2048]{1,0:T(8,128)(2,1)S(1)}, bf16[128,2048]{1,0:T(8,128)(2,1)}, u32[]{:S(2)}) copy-start(bf16[128,2048]{1,0:T(8,128)(2,1)} %param.7) | copy-start | bytes 1572868
  7.9 123.4 %all-gather.4.cloned.1.call-start = ((), (), s32[]{:S(2)}) async-start(), calls=%async_computation.3 | async-start | bytes 7864320 | tf_op jit(solution)/shard_map/all_gather | solution.py:58
  17.8 109.2 %all-to-all-start = ((bf16[64,8,4096]{2,1,0:T(8,128)(2,1)}), bf16[64,8,4096]{2,1,0:T(8,128)(2,1)}, u32[]{:S(2)}, u32[]{:S(2)}) async-start(bf16[64,8,4096]{2,1,0:T(8,128)(2,1)} %bitcast.55), calls=%async_computation | async-start | bytes 8388608 | tf_op jit(solution)/shard_map/all_to_all | solution.py:55
  31.1 212.0 %reduce-scatter.2.cloned.1.call-start = ((), (), s32[]{:S(2)}) async-start(), calls=%async_computation.4 | async-start | bytes 11796480 | tf_op jit(solution)/shard_map/reduce_scatter | solution.py:75
  131.3 4.5 %copy-start.4 = (bf16[2,2048,768]{2,1,0:T(8,128)(2,1)S(1)}, bf16[2,2048,768]{2,1,0:T(8,128)(2,1)}, u32[]{:S(2)}) copy-start(bf16[2,2048,768]{2,1,0:T(8,128)(2,1)} %all-gather.4.cloned.1.call-done) | copy-start | bytes 18874372
  163.9 57.0 %all-to-all-start.1 = ((bf16[64,8,2048]{2,1,0:T(8,128)(2,1)}), bf16[64,8,2048]{2,1,0:T(8,128)(2,1)S(1)}, u32[]{:S(2)}, u32[]{:S(2)}) async-start(bf16[64,8,2048]{2,1,0:T(8,128)(2,1)} %fusion.8), calls=%async_computation.2 | async-start | bytes 4194304 | tf_op jit(solution)/shard_map/all_to_all | solution.py:72
Sparse Core Ops, SparseCore 0:
  9.8 45.6 all-gather.5
  57.9 68.3 all-gather.3
  155.2 87.9 reduce-scatter.1

commit v8 on v4

--- a/solution.py
+++ b/solution.py
@@ -60,8 +60,12 @@
         jnp.stack([w_gate[0], w_up[0], w_down[0]], axis=0), "rep", axis=1, tiled=True
     )
     full_gate, full_up, full_down = full_all[0], full_all[1], full_all[2]
-    pre_gate = jnp.dot(x_recv, full_gate, preferred_element_type=jnp.float32)
-    pre_up = jnp.dot(x_recv, full_up, preferred_element_type=jnp.float32)
+    ff = full_gate.shape[1]
+    pre_both = jnp.dot(
+        x_recv, jnp.concatenate([full_gate, full_up], axis=1), preferred_element_type=jnp.float32
+    )
+    pre_gate = pre_both[:, :ff]
+    pre_up = pre_both[:, ff:]
     hid_grad = jnp.dot(g_recv, full_down, preferred_element_type=jnp.float32)
     sig_gate = jax.nn.sigmoid(pre_gate)
     silu_gate = pre_gate * sig_gate

time: 250 us -> 253 us (1.012)
  blocking collectives: 109 us -> 0 us
  waiting for transfers between devices: 67.8 us -> 159 us
  starting transfers between devices: 5.91 us -> 19.3 us
  local copies, waits for them, and re-layouts: 12.6 us -> 17.5 us
  matrix products: 26.7 us -> 29.9 us
    all_to_all x1 -> x0, blocking collectives: 109 us -> none  [per_device(): lax.all_to_all(table[by_choice], 'exp', split_axis=0, concat_axis=0, tile...]
    all_gather x1, waiting for transfers between devices: 0.01 us -> 76.3 us  [per_device(): lax.all_gather(jnp.stack([w_gate[0], w_up[0], w_down[0]], axis=0), 'rep',...]
    all_to_all x0 -> x1, waiting for transfers between devices: none -> 14.4 us  [per_device(): lax.all_to_all(table[by_choice], 'exp', split_axis=0, concat_axis=0, tile...]
    all_to_all x0 -> x1, starting transfers between devices: none -> 13.3 us  [per_device(): lax.all_to_all(table[by_choice], 'exp', split_axis=0, concat_axis=0, tile...]
    squeeze x0 -> x1, local copies, waits for them, and re-layouts: none -> 4.86 us  [per_device(): full_gate, full_up, full_down = (full_all[0], full_all[1], full_all[2])]
    dot_general x3, matrix products: 5.62 us -> 10.4 us  [contract_rows(): lax.dot_general(left, right, (((0,), (0,)), ((), ())), preferred_element_...]
    dot_general x2 -> x1, matrix products: 8.58 us -> 5.93 us  [per_device(): jnp.dot(x_recv, jnp.concatenate([full_gate, full_up], axis=1), preferred_...]
  transfers between devices with their start and end apart: 3 -> 4, of which waited for: 2 -> 4; matrix products, arithmetic and copies ran while one was open for 9% -> 11% of each run, Pallas kernels for 0% -> 0%
where the time goes in v8:
time: 253 us
  waiting for transfers between devices  159 us (63%)
  matrix products  29.9 us (12%)
  starting transfers between devices  19.3 us (8%)
  local copies, waits for them, and re-layouts  17.5 us (7%)
  between operations  14.3 us (6%)
  other arithmetic  13.3 us (5%)
    all_gather x1, waiting for transfers between devices, per_device(): lax.all_gather(jnp.stack([w_gate[0], w_up[0], w_down[0]], axis=0), 'rep',...  76.3 us
    all_to_all x1, waiting for transfers between devices, per_device(): lax.all_to_all(row_grad, 'exp', split_axis=0, concat_axis=0, tiled=True)  51.2 us
    reduce_scatter x1, waiting for transfers between devices, per_device(): lax.psum_scatter(jnp.stack([contract_rows(x_recv, d_gate), contract_rows(...  16.6 us
    all_to_all x1, waiting for transfers between devices, per_device(): lax.all_to_all(table[by_choice], 'exp', split_axis=0, concat_axis=0, tile...  14.4 us
    all_to_all x1, starting transfers between devices, per_device(): lax.all_to_all(table[by_choice], 'exp', split_axis=0, concat_axis=0, tile...  13.3 us
    dot_general x3, matrix products, contract_rows(): lax.dot_general(left, right, (((0,), (0,)), ((), ())), preferred_element_...  10.4 us
    dot_general x2, matrix products, against_cols(): lax.dot_general(left, right, (((1,), (1,)), ((), ())), preferred_element_...  8.81 us
    dot_general x1, matrix products, per_device(): jnp.dot(x_recv, jnp.concatenate([full_gate, full_up], axis=1), preferred_...  5.93 us
  transfers between devices with their start and end apart: 4, of which 4 were waited for; matrix products, arithmetic and copies ran while one was open for 11% of the time, Pallas kernels for 0%

profile of v8, /device:TPU:1, one launch (start us, length us, event | category | flops | bytes accessed | tf_op | source)
XLA Modules:
  0.0 252.8 jit_solution(4947512938447528919)
XLA Ops:
  7.2 0.0 copy-start.2
  7.2 0.0 copy-start.3
  7.2 0.0 copy-start
  7.2 0.0 all-gather.2.cloned.1.call-start
  7.2 3.3 %pad_maximum_fusion.1 = bf16[3,512,768]{2,1,0:T(8,128)(2,1)} fusion(bf16[1,512,768]{2,1,0:T(8,128)(2,1)} %param.13, bf16[1,512,768]{2,1,0:T(8,128)(2,1)} %param.12, bf16[1,512,768]{2,1,0:T(8,128)(2,1)} %param.11), kind=kLoop, calls=%fused_computation.20 | loop fusion | flops 2359296 | bytes 4718592 | tf_op jit(solution)/shard_map/stack | solution.py:60
  10.6 0.0 copy-start.1
  10.6 0.0 all-gather.2.cloned.1.call-update
  10.6 0.0 copy-done.2
  10.6 0.1 copy.12
  10.7 0.1 eq.31
  10.9 0.1 eq.27
  11.0 0.6 reduce-window.6
  11.6 0.2 slice_reduce_fusion
  11.9 0.1 copy.11
  12.0 0.1 mul.74
  12.1 0.1 fusion.19
  12.3 1.4 scatter_custom_fusion
  13.7 0.0 copy-done.3
  13.7 0.0 copy-done
  13.7 0.2 fusion.15
  14.0 0.0 copy-done.1
  14.0 0.6 maximum_maximum_fusion
  14.6 4.4 %gather_fusion = bf16[512,4096]{1,0:T(8,128)(2,1)} fusion(bf16[257,4096]{1,0:T(8,128)(2,1)S(1)} %maximum_maximum_fusion, s32[1024]{0:T(1024)S(1)} %pad_clamp_fusion.1), kind=kCustom, calls=%fused_computation | custom fusion | bytes 8390656 | tf_op jit(solution)/shard_map/gather | solution.py:56
  18.9 13.3 %all-to-all-start = ((bf16[64,8,4096]{2,1,0:T(8,128)(2,1)}), bf16[64,8,4096]{2,1,0:T(8,128)(2,1)}, u32[]{:S(2)}, u32[]{:S(2)}) async-start(bf16[64,8,4096]{2,1,0:T(8,128)(2,1)} %bitcast.49), calls=%async_computation | async-start | bytes 8388608 | tf_op jit(solution)/shard_map/all_to_all | solution.py:56
  32.3 0.2 reduce-scatter.2.cloned.1.call-start
  32.5 76.3 %all-gather.2.cloned.1.call-done = bf16[3,2048,768]{2,1,0:T(8,128)(2,1)} async-done(((bf16[3,512,768]{2,1,0:T(8,128)(2,1)}), bf16[3,2048,768]{2,1,0:T(8,128)(2,1)}) %all-gather.2.cloned.1.call-update) | async-done | bytes 9437200 | tf_op jit(solution)/shard_map/all_gather | solution.py:59
  108.8 4.9 %slice_bitcast_fusion.1 = (bf16[2048,768]{1,0:T(8,128)(2,1)S(1)}, bf16[2048,768]{1,0:T(8,128)(2,1)}) fusion(bf16[3,2048,768]{2,1,0:T(8,128)(2,1)} %all-gather.2.cloned.1.call-done), kind=kLoop, calls=%fused_computation.13 | loop fusion | bytes 12582912 | tf_op jit(solution)/shard_map/squeeze | solution.py:62
  113.7 14.4 %all-to-all-done = bf16[64,8,4096]{2,1,0:T(8,128)(2,1)} async-done(((bf16[64,8,4096]{2,1,0:T(8,128)(2,1)}), bf16[64,8,4096]{2,1,0:T(8,128)(2,1)}, u32[]{:S(2)}, u32[]{:S(2)}) %all-to-all-start) | async-done | bytes 4194336 | tf_op jit(solution)/shard_map/all_to_all | solution.py:56
  128.1 5.9 %fusion = f32[512,1536]{1,0:T(8,128)S(1)} fusion(bf16[2048,768]{1,0:T(8,128)(2,1)} %get-tuple-element.5, bf16[2048,768]{1,0:T(8,128)(2,1)S(1)} %get-tuple-element.4, bf16[512,4096]{1,0:T(8,128)(2,1)} %bitcast.6), kind=kOutput, calls=%fused_computation.4 | convolution fusion | flops 3233808384 | bytes 11534336 | tf_op jit(solution)/shard_map/dot_general | solution.py:64
  134.1 3.6 %fusion.7 = bf16[1,2048,768]{2,1,0:T(8,128)(2,1)S(1)} fusion(bf16[512,4096]{1,0:T(8,128)(2,1)} %bitcast.6, f32[512,1536]{1,0:T(8,128)S(1)} %fusion), kind=kOutput, calls=%fused_computation.18 | convolution fusion | flops 1614544896 | bytes 8388608 | tf_op jit(solution)/shard_map/dot_general | solution.py:8
  137.6 4.7 %multiply_convert_fusion.2 = (bf16[512,768]{1,0:T(8,128)(2,1)S(1)}, bf16[512,768]{1,0:T(8,128)(2,1)S(1)}) fusion(f32[512,1536]{1,0:T(8,128)S(1)} %fusion, bf16[3,2048,768]{2,1,0:T(8,128)(2,1)} %all-gather.2.cloned.1.call-done, bf16[512,4096]{1,0:T(8,128)(2,1)} %bitcast.6), kind=kOutput, calls=%fused_computation.29 | convolution fusion | flops 1615724544 | bytes 9961472 | tf_op jit(solution)/shard_map/dot_general | solution.py:69
  142.4 3.4 %fusion.5 = bf16[1,2048,768]{2,1,0:T(8,128)(2,1)S(1)} fusion(bf16[512,768]{1,0:T(8,128)(2,1)S(1)} %get-tuple-element.6, bf16[512,4096]{1,0:T(8,128)(2,1)} %bitcast.6), kind=kOutput, calls=%fused_computation.16 | convolution fusion | flops 1612185600 | bytes 6029312 | tf_op jit(solution)/shard_map/dot_general | solution.py:8
  145.8 3.4 %fusion.6 = bf16[1,2048,768]{2,1,0:T(8,128)(2,1)S(1)} fusion(bf16[512,768]{1,0:T(8,128)(2,1)S(1)} %get-tuple-element.7, bf16[512,4096]{1,0:T(8,128)(2,1)} %bitcast.6), kind=kOutput, calls=%fused_computation.17 | convolution fusion | flops 1612185600 | bytes 6029312 | tf_op jit(solution)/shard_map/dot_general | solution.py:8
  149.2 4.7 %pad_maximum_fusion = bf16[3,2048,768]{2,1,0:T(8,128)(2,1)} fusion(bf16[1,2048,768]{2,1,0:T(8,128)(2,1)S(1)} %fusion.7, bf16[1,2048,768]{2,1,0:T(8,128)(2,1)S(1)} %fusion.6, bf16[1,2048,768]{2,1,0:T(8,128)(2,1)S(1)} %fusion.5), kind=kLoop, calls=%fused_computation.3 | loop fusion | flops 9437184 | bytes 18874368 | tf_op jit(solution)/shard_map/stack | solution.py:82
  153.9 0.0 reduce-scatter.2.cloned.1.call-update
  154.0 3.7 %fusion.30 = f32[512,2048]{1,0:T(8,128)S(1)} fusion(bf16[512,768]{1,0:T(8,128)(2,1)S(1)} %get-tuple-element.6, bf16[3,2048,768]{2,1,0:T(8,128)(2,1)} %all-gather.2.cloned.1.call-done), kind=kOutput, calls=%fused_computation.66 | convolution fusion | flops 1610612736 | bytes 8126464 | tf_op jit(solution)/shard_map/dot_general | solution.py:14
  157.7 5.1 %fusion.8 = bf16[64,8,2048]{2,1,0:T(8,128)(2,1)} fusion(f32[512,2048]{1,0:T(8,128)S(1)} %fusion.30, bf16[512,768]{1,0:T(8,128)(2,1)S(1)} %get-tuple-element.7, bf16[3,2048,768]{2,1,0:T(8,128)(2,1)} %all-gather.2.cloned.1.call-done), kind=kOutput, calls=%fused_computation.19 | convolution fusion | flops 1612709888 | bytes 10223616 | tf_op jit(solution)/shard_map/dot_general | solution.py:14
  162.8 5.7 %all-to-all-start.1 = ((bf16[64,8,2048]{2,1,0:T(8,128)(2,1)}), bf16[64,8,2048]{2,1,0:T(8,128)(2,1)S(1)}, u32[]{:S(2)}, u32[]{:S(2)}) async-start(bf16[64,8,2048]{2,1,0:T(8,128)(2,1)} %fusion.8), calls=%async_computation.2 | async-start | bytes 4194304 | tf_op jit(solution)/shard_map/all_to_all | solution.py:78
  168.5 51.2 %all-to-all-done.1 = bf16[64,8,2048]{2,1,0:T(8,128)(2,1)S(1)} async-done(((bf16[64,8,2048]{2,1,0:T(8,128)(2,1)}), bf16[64,8,2048]{2,1,0:T(8,128)(2,1)S(1)}, u32[]{:S(2)}, u32[]{:S(2)}) %all-to-all-start.1) | async-done | bytes 2097184 | tf_op jit(solution)/shard_map/all_to_all | solution.py:78
  219.7 1.4 gather_fusion.1
  221.1 0.7 reshape.64
  221.8 3.6 %reduce_sum.25 = bf16[128,2048]{1,0:T(8,128)(2,1)} reduce(bf16[128,2,2048]{2,1,0:T(2,128)(2,1)S(1)} %reshape.64, bf16[]{:T(256)} %constant.41.clone.1), dimensions={1}, to_apply=%region_5.6 | reduce | flops 262144 | bytes 1572866 | tf_op jit(solution)/shard_map/reduce_sum | solution.py:80
  225.5 16.6 %reduce-scatter.2.cloned.1.call-done = bf16[3,512,768]{2,1,0:T(8,128)(2,1)} async-done(((bf16[3,2048,768]{2,1,0:T(8,128)(2,1)}), bf16[3,512,768]{2,1,0:T(8,128)(2,1)}) %reduce-scatter.2.cloned.1.call-update) | async-done | bytes 2359312 | tf_op jit(solution)/shard_map/reduce_scatter | solution.py:81
  242.1 3.9 %fusion.31 = (f32[1,512,768]{2,1,0:T(8,128)}, f32[1,512,768]{2,1,0:T(8,128)}, f32[1,512,768]{2,1,0:T(8,128)}) fusion(bf16[3,512,768]{2,1,0:T(8,128)(2,1)} %reduce-scatter.2.cloned.1.call-done), kind=kLoop, calls=%fused_computation.67 | loop fusion | bytes 9437184 | tf_op jit(solution)/shard_map/slice | solution.py:97
  (11 shorter events, 0.1 us)
Async XLA Ops:
  7.2 3.4 %copy-start.2 = (s32[128,2]{0,1:T(2,128)S(1)}, s32[128,2]{0,1:T(2,128)}, u32[]{:S(2)}) copy-start(s32[128,2]{0,1:T(2,128)} %param.9) | copy-start | bytes 3076
  7.2 6.5 %copy-start.3 = (f32[128,2]{0,1:T(2,128)S(1)}, f32[128,2]{0,1:T(2,128)}, u32[]{:S(2)}) copy-start(f32[128,2]{0,1:T(2,128)} %param.10) | copy-start | bytes 3076
  7.2 6.5 %copy-start = (bf16[128,2048]{1,0:T(8,128)(2,1)S(1)}, bf16[128,2048]{1,0:T(8,128)(2,1)}, u32[]{:S(2)}) copy-start(bf16[128,2048]{1,0:T(8,128)(2,1)} %param.8) | copy-start | bytes 1572868
  7.2 101.6 %all-gather.2.cloned.1.call-start = ((), (), s32[]{:S(2)}) async-start(), calls=%async_computation.3 | async-start | bytes 11796480 | tf_op jit(solution)/shard_map/all_gather | solution.py:59
  10.6 3.4 %copy-start.1 = (bf16[128,2048]{1,0:T(8,128)(2,1)S(1)}, bf16[128,2048]{1,0:T(8,128)(2,1)}, u32[]{:S(2)}) copy-start(bf16[128,2048]{1,0:T(8,128)(2,1)} %param.7) | copy-start | bytes 1572868
  18.9 109.2 %all-to-all-start = ((bf16[64,8,4096]{2,1,0:T(8,128)(2,1)}), bf16[64,8,4096]{2,1,0:T(8,128)(2,1)}, u32[]{:S(2)}, u32[]{:S(2)}) async-start(bf16[64,8,4096]{2,1,0:T(8,128)(2,1)} %bitcast.49), calls=%async_computation | async-start | bytes 8388608 | tf_op jit(solution)/shard_map/all_to_all | solution.py:56
  32.3 209.8 %reduce-scatter.2.cloned.1.call-start = ((), (), s32[]{:S(2)}) async-start(), calls=%async_computation.4 | async-start | bytes 11796480 | tf_op jit(solution)/shard_map/reduce_scatter | solution.py:81
  162.8 57.0 %all-to-all-start.1 = ((bf16[64,8,2048]{2,1,0:T(8,128)(2,1)}), bf16[64,8,2048]{2,1,0:T(8,128)(2,1)S(1)}, u32[]{:S(2)}, u32[]{:S(2)}) async-start(bf16[64,8,2048]{2,1,0:T(8,128)(2,1)} %fusion.8), calls=%async_computation.2 | async-start | bytes 4194304 | tf_op jit(solution)/shard_map/all_to_all | solution.py:78
Sparse Core Ops, SparseCore 0:
  10.7 98.0 all-gather.1
  154.1 87.9 reduce-scatter.1

commit v9 on v7

--- a/solution.py
+++ b/solution.py
@@ -55,9 +55,10 @@
     both_recv = lax.all_to_all(table[by_choice], "exp", split_axis=0, concat_axis=0, tiled=True)
     x_recv = both_recv[:, :model_width]
     g_recv = both_recv[:, model_width:]
-    gate_up = lax.all_gather(jnp.stack([w_gate[0], w_up[0]], axis=0), "rep", axis=1, tiled=True)
-    full_gate, full_up = gate_up[0], gate_up[1]
-    full_down = lax.all_gather(w_down[0], "rep", axis=0, tiled=True)
+    full_all = lax.all_gather(
+        jnp.stack([w_gate[0], w_up[0], w_down[0]], axis=0), "rep", axis=1, tiled=True
+    )
+    full_gate, full_up, full_down = full_all[0], full_all[1], full_all[2]
     pre_gate = jnp.dot(x_recv, full_gate, preferred_element_type=jnp.float32)
     pre_up = jnp.dot(x_recv, full_up, preferred_element_type=jnp.float32)
     hid_grad = jnp.dot(g_recv, full_down, preferred_element_type=jnp.float32)

time: 254 us -> 249 us (0.980)
  blocking collectives: 0 us -> 109 us
  waiting for transfers between devices: 164 us -> 67.5 us
  starting transfers between devices: 19.4 us -> 5.9 us
  matrix products: 32 us -> 26.7 us
    all_to_all x0 -> x1, blocking collectives: none -> 109 us  [per_device(): lax.all_to_all(table[by_choice], 'exp', split_axis=0, concat_axis=0, tile...]
    all_to_all x1 -> x0, waiting for transfers between devices: 71.5 us -> none  [per_device(): lax.all_to_all(table[by_choice], 'exp', split_axis=0, concat_axis=0, tile...]
    all_gather x2 -> x1, waiting for transfers between devices: 24.2 us -> 0.01 us  [per_device(): lax.all_gather(jnp.stack([w_gate[0], w_up[0], w_down[0]], axis=0), 'rep',...]
    all_to_all x1 -> x0, starting transfers between devices: 13.3 us -> none  [per_device(): lax.all_to_all(table[by_choice], 'exp', split_axis=0, concat_axis=0, tile...]
    dot_general x3, matrix products: 10.4 us -> 5.62 us  [contract_rows(): lax.dot_general(left, right, (((0,), (0,)), ((), ())), preferred_element_...]
  transfers between devices with their start and end apart: 5 -> 3, of which waited for: 4 -> 2; matrix products, arithmetic and copies ran while one was open for 11% -> 9% of each run, Pallas kernels for 0% -> 0%
where the time goes in v9:
time: 249 us; the launch traced here: 248 us
  blocking collectives  109 us (44%)
  waiting for transfers between devices  67.5 us (27%)
  matrix products  26.7 us (11%)
  between operations  14.3 us (6%)
  other arithmetic  13.4 us (5%)
  local copies, waits for them, and re-layouts  11.2 us (4%)
  starting transfers between devices  5.9 us (2%)
    all_to_all x1, blocking collectives, per_device(): lax.all_to_all(table[by_choice], 'exp', split_axis=0, concat_axis=0, tile...  109 us
    all_to_all x1, waiting for transfers between devices, per_device(): lax.all_to_all(row_grad, 'exp', split_axis=0, concat_axis=0, tiled=True)  50.9 us
    reduce_scatter x1, waiting for transfers between devices, per_device(): lax.psum_scatter(jnp.stack([contract_rows(x_recv, d_gate), contract_rows(...  16.5 us
    dot_general x2, matrix products, against_cols(): lax.dot_general(left, right, (((1,), (1,)), ((), ())), preferred_element_...  8.81 us
    all_to_all x1, starting transfers between devices, per_device(): lax.all_to_all(row_grad, 'exp', split_axis=0, concat_axis=0, tiled=True)  5.82 us
    dot_general x3, matrix products, contract_rows(): lax.dot_general(left, right, (((0,), (0,)), ((), ())), preferred_element_...  5.62 us
  transfers between devices with their start and end apart: 3, of which 2 were waited for; matrix products, arithmetic and copies ran while one was open for 9% of the time, Pallas kernels for 0%

profile of v9, /device:TPU:1, one launch (start us, length us, event | category | flops | bytes accessed | tf_op | source)
XLA Modules:
  0.0 248.3 jit_solution(10008156442834694363)
XLA Ops:
  7.2 0.0 copy-start.3
  7.2 0.0 copy-start.4
  7.2 0.0 copy-start.1
  7.2 0.0 all-gather.2.cloned.1.call-start
  7.2 3.3 %pad_maximum_fusion.1 = bf16[3,512,768]{2,1,0:T(8,128)(2,1)} fusion(bf16[1,512,768]{2,1,0:T(8,128)(2,1)} %param.13, bf16[1,512,768]{2,1,0:T(8,128)(2,1)} %param.12, bf16[1,512,768]{2,1,0:T(8,128)(2,1)} %param.11), kind=kLoop, calls=%fused_computation.18 | loop fusion | flops 2359296 | bytes 4718592 | tf_op jit(solution)/shard_map/stack | solution.py:59
  10.6 0.0 copy-start.2
  10.6 0.0 all-gather.2.cloned.1.call-update
  10.6 0.0 reduce-scatter.2.cloned.1.call-start
  10.6 0.0 copy-done.3
  10.6 0.1 copy.15
  10.8 0.1 eq.41
  10.9 0.1 reshape.176
  11.1 0.6 reduce-window.6
  11.7 0.2 slice_reduce_fusion
  11.9 0.1 fusion.20
  12.0 0.2 fusion.17
  12.2 0.2 select_reduce_fusion
  12.4 0.0 copy-done.4
  12.4 0.0 copy-done.1
  12.4 0.2 fusion.15
  12.7 0.0 copy-done.2
  12.7 0.6 maximum_maximum_fusion
  13.3 4.4 %gather_fusion = bf16[512,4096]{1,0:T(8,128)(2,1)} fusion(bf16[257,4096]{1,0:T(8,128)(2,1)S(1)} %maximum_maximum_fusion, s32[1024]{0:T(1024)S(1)} %pad_clamp_fusion.1), kind=kCustom, calls=%fused_computation | custom fusion | bytes 8390656 | tf_op jit(solution)/shard_map/gather | solution.py:55
  17.6 109.4 %all_to_all.24 = bf16[64,8,4096]{2,1,0:T(8,128)(2,1)} all-to-all(bf16[64,8,4096]{2,1,0:T(8,128)(2,1)} %bitcast.55), channel_id=1, replica_groups=mesh['rep'=4,'exp'=64] {'exp'}, dimensions={0} | all-to-all | bytes 8388608 | tf_op jit(solution)/shard_map/all_to_all | solution.py:55
  127.0 0.0 all-gather.2.cloned.1.call-done
  127.0 0.0 copy-start
  127.0 4.5 %fusion.4 = f32[512,768]{1,0:T(8,128)S(1)} fusion(bf16[3,2048,768]{2,1,0:T(8,128)(2,1)} %all-gather.2.cloned.1.call-done, bf16[512,4096]{1,0:T(8,128)(2,1)} %bitcast.56), kind=kOutput, calls=%fused_computation.14 | convolution fusion | flops 1610612736 | bytes 6815744 | tf_op jit(solution)/shard_map/dot_general | solution.py:63
  131.5 0.0 copy-done
  131.5 3.7 %fusion = f32[512,768]{1,0:T(8,128)S(1)} fusion(bf16[3,2048,768]{2,1,0:T(8,128)(2,1)} %all-gather.2.cloned.1.call-done, bf16[512,4096]{1,0:T(8,128)(2,1)S(1)} %bitcast.57), kind=kOutput, calls=%fused_computation.10 | convolution fusion | flops 1610612736 | bytes 6815744 | tf_op jit(solution)/shard_map/dot_general | solution.py:64
  135.2 4.1 %multiply_convert_fusion.2 = (bf16[512,768]{1,0:T(8,128)(2,1)S(1)}, bf16[512,768]{1,0:T(8,128)(2,1)S(1)}, f32[512,768]{1,0:T(8,128)S(1)}) fusion(f32[512,768]{1,0:T(8,128)S(1)} %fusion, f32[512,768]{1,0:T(8,128)S(1)} %fusion.4, bf16[3,2048,768]{2,1,0:T(8,128)(2,1)} %all-gather.2.cloned.1.call-done, bf16[512,4096]{1,0:T(8,128)(2,1)S(1)} %bitcast.58), kind=kOutput, calls=%fused_computation.24 | convolution fusion | flops 1615724544 | bytes 11534336 | tf_op jit(solution)/shard_map/dot_general | solution.py:62
  139.3 1.8 fusion.1
  141.2 1.8 fusion.2
  143.0 1.9 fusion.3
  145.0 4.5 %pad_maximum_fusion = bf16[3,2048,768]{2,1,0:T(8,128)(2,1)} fusion(bf16[1,2048,768]{2,1,0:T(8,128)(2,1)S(1)} %fusion.3, bf16[1,2048,768]{2,1,0:T(8,128)(2,1)S(1)} %fusion.2, bf16[1,2048,768]{2,1,0:T(8,128)(2,1)S(1)} %fusion.1), kind=kLoop, calls=%fused_computation.2 | loop fusion | flops 9437184 | bytes 18874368 | tf_op jit(solution)/shard_map/stack | solution.py:77
  149.5 0.0 reduce-scatter.2.cloned.1.call-update
  149.5 3.7 %fusion.5 = f32[512,2048]{1,0:T(8,128)S(1)} fusion(bf16[512,768]{1,0:T(8,128)(2,1)S(1)} %get-tuple-element.4, bf16[3,2048,768]{2,1,0:T(8,128)(2,1)} %all-gather.2.cloned.1.call-done), kind=kOutput, calls=%fused_computation.15 | convolution fusion | flops 1610612736 | bytes 8126464 | tf_op jit(solution)/shard_map/dot_general | solution.py:14
  153.2 5.1 %fusion.7 = bf16[64,8,2048]{2,1,0:T(8,128)(2,1)} fusion(f32[512,2048]{1,0:T(8,128)S(1)} %fusion.5, bf16[512,768]{1,0:T(8,128)(2,1)S(1)} %get-tuple-element.5, bf16[3,2048,768]{2,1,0:T(8,128)(2,1)} %all-gather.2.cloned.1.call-done), kind=kOutput, calls=%fused_computation.17 | convolution fusion | flops 1612709888 | bytes 10223616 | tf_op jit(solution)/shard_map/dot_general | solution.py:14
  158.3 5.8 %all-to-all-start.1 = ((bf16[64,8,2048]{2,1,0:T(8,128)(2,1)}), bf16[64,8,2048]{2,1,0:T(8,128)(2,1)S(1)}, u32[]{:S(2)}, u32[]{:S(2)}) async-start(bf16[64,8,2048]{2,1,0:T(8,128)(2,1)} %fusion.7), calls=%async_computation.2 | async-start | bytes 4194304 | tf_op jit(solution)/shard_map/all_to_all | solution.py:73
  164.2 0.1 copy.18
  164.3 0.1 mul.101
  164.4 50.9 %all-to-all-done.1 = bf16[64,8,2048]{2,1,0:T(8,128)(2,1)S(1)} async-done(((bf16[64,8,2048]{2,1,0:T(8,128)(2,1)}), bf16[64,8,2048]{2,1,0:T(8,128)(2,1)S(1)}, u32[]{:S(2)}, u32[]{:S(2)}) %all-to-all-start.1) | async-done | bytes 2097184 | tf_op jit(solution)/shard_map/all_to_all | solution.py:73
  215.4 1.4 gather_fusion.1
  216.7 0.7 reshape.178
  217.4 3.6 %reduce_sum.35 = bf16[128,2048]{1,0:T(8,128)(2,1)} reduce(bf16[128,2,2048]{2,1,0:T(2,128)(2,1)S(1)} %reshape.178, bf16[]{:T(256)} %constant.42.clone.1), dimensions={1}, to_apply=%region_6.7 | reduce | flops 262144 | bytes 1572866 | tf_op jit(solution)/shard_map/reduce_sum | solution.py:75
  221.1 16.5 %reduce-scatter.2.cloned.1.call-done = bf16[3,512,768]{2,1,0:T(8,128)(2,1)} async-done(((bf16[3,2048,768]{2,1,0:T(8,128)(2,1)}), bf16[3,512,768]{2,1,0:T(8,128)(2,1)}) %reduce-scatter.2.cloned.1.call-update) | async-done | bytes 2359312 | tf_op jit(solution)/shard_map/reduce_scatter | solution.py:76
  237.6 3.9 %fusion.25 = (f32[1,512,768]{2,1,0:T(8,128)}, f32[1,512,768]{2,1,0:T(8,128)}, f32[1,512,768]{2,1,0:T(8,128)}) fusion(bf16[3,512,768]{2,1,0:T(8,128)(2,1)} %reduce-scatter.2.cloned.1.call-done), kind=kLoop, calls=%fused_computation.64 | loop fusion | bytes 9437184 | tf_op jit(solution)/shard_map/slice | solution.py:92
  (12 shorter events, 0.1 us)
Async XLA Ops:
  7.2 3.5 %copy-start.3 = (s32[128,2]{0,1:T(2,128)S(1)}, s32[128,2]{0,1:T(2,128)}, u32[]{:S(2)}) copy-start(s32[128,2]{0,1:T(2,128)} %param.9) | copy-start | bytes 3076
  7.2 5.2 %copy-start.4 = (f32[128,2]{0,1:T(2,128)S(1)}, f32[128,2]{0,1:T(2,128)}, u32[]{:S(2)}) copy-start(f32[128,2]{0,1:T(2,128)} %param.10) | copy-start | bytes 3076
  7.2 5.2 %copy-start.1 = (bf16[128,2048]{1,0:T(8,128)(2,1)S(1)}, bf16[128,2048]{1,0:T(8,128)(2,1)}, u32[]{:S(2)}) copy-start(bf16[128,2048]{1,0:T(8,128)(2,1)} %param.8) | copy-start | bytes 1572868
  7.2 119.8 %all-gather.2.cloned.1.call-start = ((), (), s32[]{:S(2)}) async-start(), calls=%async_computation.3 | async-start | bytes 11796480 | tf_op jit(solution)/shard_map/all_gather | solution.py:58
  10.6 2.1 copy-start.2
  10.6 227.0 %reduce-scatter.2.cloned.1.call-start = ((), (), s32[]{:S(2)}) async-start(), calls=%async_computation.4 | async-start | bytes 11796480 | tf_op jit(solution)/shard_map/reduce_scatter | solution.py:76
  127.0 4.5 %copy-start = (bf16[64,8,4096]{2,1,0:T(8,128)(2,1)S(1)}, bf16[64,8,4096]{2,1,0:T(8,128)(2,1)}, u32[]{:S(2)}) copy-start(bf16[64,8,4096]{2,1,0:T(8,128)(2,1)} %all_to_all.24) | copy-start | bytes 12582916
  158.3 57.0 %all-to-all-start.1 = ((bf16[64,8,2048]{2,1,0:T(8,128)(2,1)}), bf16[64,8,2048]{2,1,0:T(8,128)(2,1)S(1)}, u32[]{:S(2)}, u32[]{:S(2)}) async-start(bf16[64,8,2048]{2,1,0:T(8,128)(2,1)} %fusion.7), calls=%async_computation.2 | async-start | bytes 4194304 | tf_op jit(solution)/shard_map/all_to_all | solution.py:73
Sparse Core Ops, SparseCore 0:
  10.7 98.0 all-gather.1
  149.6 87.9 reduce-scatter.1

commit v10 on v9

--- a/solution.py
+++ b/solution.py
@@ -59,8 +59,11 @@
         jnp.stack([w_gate[0], w_up[0], w_down[0]], axis=0), "rep", axis=1, tiled=True
     )
     full_gate, full_up, full_down = full_all[0], full_all[1], full_all[2]
-    pre_gate = jnp.dot(x_recv, full_gate, preferred_element_type=jnp.float32)
-    pre_up = jnp.dot(x_recv, full_up, preferred_element_type=jnp.float32)
+    pre_both = lax.dot_general(
+        x_recv, full_all[0:2], (((1,), (1,)), ((), ())), preferred_element_type=jnp.float32
+    )
+    pre_gate = pre_both[:, 0, :]
+    pre_up = pre_both[:, 1, :]
     hid_grad = jnp.dot(g_recv, full_down, preferred_element_type=jnp.float32)
     sig_gate = jax.nn.sigmoid(pre_gate)
     silu_gate = pre_gate * sig_gate

time: 249 us -> 247 us (level)
    dot_general x2 -> x1, matrix products: 8.59 us -> 6.36 us  [per_device(): lax.dot_general(x_recv, full_all[0:2], (((1,), (1,)), ((), ())), preferre...]
where the time goes in v10:
time: 247 us
  blocking collectives  109 us (44%)
  waiting for transfers between devices  67.3 us (27%)
  matrix products  25 us (10%)
  between operations  14.3 us (6%)
  other arithmetic  13.4 us (5%)
  local copies, waits for them, and re-layouts  11.2 us (5%)
  starting transfers between devices  6.13 us (2%)
    all_to_all x1, blocking collectives, per_device(): lax.all_to_all(table[by_choice], 'exp', split_axis=0, concat_axis=0, tile...  109 us
    all_to_all x1, waiting for transfers between devices, per_device(): lax.all_to_all(row_grad, 'exp', split_axis=0, concat_axis=0, tiled=True)  50.9 us
    reduce_scatter x1, waiting for transfers between devices, per_device(): lax.psum_scatter(jnp.stack([contract_rows(x_recv, d_gate), contract_rows(...  16.3 us
    dot_general x2, matrix products, against_cols(): lax.dot_general(left, right, (((1,), (1,)), ((), ())), preferred_element_...  8.81 us
    dot_general x1, matrix products, per_device(): lax.dot_general(x_recv, full_all[0:2], (((1,), (1,)), ((), ())), preferre...  6.36 us
    all_to_all x1, starting transfers between devices, per_device(): lax.all_to_all(row_grad, 'exp', split_axis=0, concat_axis=0, tiled=True)  6.05 us
    dot_general x3, matrix products, contract_rows(): lax.dot_general(left, right, (((0,), (0,)), ((), ())), preferred_element_...  5.71 us
  transfers between devices with their start and end apart: 3, of which 2 were waited for; matrix products, arithmetic and copies ran while one was open for 9% of the time, Pallas kernels for 0%

profile of v10, /device:TPU:1, one launch (start us, length us, event | category | flops | bytes accessed | tf_op | source)
XLA Modules:
  0.0 246.6 jit_solution(10694857213909399074)
XLA Ops:
  7.2 0.0 copy-start.3
  7.2 0.0 copy-start.4
  7.2 0.0 copy-start.1
  7.2 0.0 all-gather.2.cloned.1.call-start
  7.2 3.3 %pad_maximum_fusion.1 = bf16[3,512,768]{2,1,0:T(8,128)(2,1)} fusion(bf16[1,512,768]{2,1,0:T(8,128)(2,1)} %param.13, bf16[1,512,768]{2,1,0:T(8,128)(2,1)} %param.12, bf16[1,512,768]{2,1,0:T(8,128)(2,1)} %param.11), kind=kLoop, calls=%fused_computation.19 | loop fusion | flops 2359296 | bytes 4718592 | tf_op jit(solution)/shard_map/stack | solution.py:59
  10.6 0.0 copy-start.2
  10.6 0.0 all-gather.2.cloned.1.call-update
  10.6 0.0 reduce-scatter.2.cloned.1.call-start
  10.6 0.0 copy-done.3
  10.6 0.1 copy.15
  10.8 0.1 eq.41
  10.9 0.1 reshape.176
  11.1 0.6 reduce-window.6
  11.7 0.2 slice_reduce_fusion
  11.9 0.1 fusion.21
  12.0 0.2 fusion.18
  12.2 0.2 select_reduce_fusion
  12.4 0.0 copy-done.4
  12.4 0.0 copy-done.1
  12.4 0.2 fusion.16
  12.7 0.0 copy-done.2
  12.7 0.6 maximum_maximum_fusion
  13.3 4.4 %gather_fusion = bf16[512,4096]{1,0:T(8,128)(2,1)} fusion(bf16[257,4096]{1,0:T(8,128)(2,1)S(1)} %maximum_maximum_fusion, s32[1024]{0:T(1024)S(1)} %pad_clamp_fusion.1), kind=kCustom, calls=%fused_computation | custom fusion | bytes 8390656 | tf_op jit(solution)/shard_map/gather | solution.py:55
  17.6 109.4 %all_to_all.24 = bf16[64,8,4096]{2,1,0:T(8,128)(2,1)} all-to-all(bf16[64,8,4096]{2,1,0:T(8,128)(2,1)} %bitcast.76), channel_id=1, replica_groups=mesh['rep'=4,'exp'=64] {'exp'}, dimensions={0} | all-to-all | bytes 8388608 | tf_op jit(solution)/shard_map/all_to_all | solution.py:55
  127.0 0.0 all-gather.2.cloned.1.call-done
  127.0 0.0 copy-start
  127.0 6.4 %fusion = f32[512,2,768]{2,0,1:T(8,128)S(1)} fusion(bf16[3,2048,768]{2,1,0:T(8,128)(2,1)} %all-gather.2.cloned.1.call-done, bf16[512,4096]{1,0:T(8,128)(2,1)} %bitcast.77), kind=kOutput, calls=%fused_computation.3 | convolution fusion | flops 3221225472 | bytes 11534336 | tf_op jit(solution)/shard_map/dot_general | solution.py:62
  133.4 0.0 copy-done
  133.4 2.0 fusion.7
  135.4 4.1 %multiply_convert_fusion.2 = (bf16[512,768]{1,0:T(8,128)(2,1)S(1)}, bf16[512,768]{1,0:T(8,128)(2,1)S(1)}) fusion(f32[512,2,768]{2,0,1:T(8,128)S(1)} %fusion, bf16[3,2048,768]{2,1,0:T(8,128)(2,1)} %all-gather.2.cloned.1.call-done, bf16[512,4096]{1,0:T(8,128)(2,1)S(1)} %bitcast.79), kind=kOutput, calls=%fused_computation.31 | convolution fusion | flops 1615724544 | bytes 9961472 | tf_op jit(solution)/shard_map/dot_general | solution.py:67
  139.5 1.9 fusion.5
  141.4 1.9 fusion.6
  143.2 4.5 %pad_maximum_fusion = bf16[3,2048,768]{2,1,0:T(8,128)(2,1)} fusion(bf16[1,2048,768]{2,1,0:T(8,128)(2,1)S(1)} %fusion.7, bf16[1,2048,768]{2,1,0:T(8,128)(2,1)S(1)} %fusion.6, bf16[1,2048,768]{2,1,0:T(8,128)(2,1)S(1)} %fusion.5), kind=kLoop, calls=%fused_computation.2 | loop fusion | flops 9437184 | bytes 18874368 | tf_op jit(solution)/shard_map/stack | solution.py:80
  147.7 0.0 reduce-scatter.2.cloned.1.call-update
  147.8 3.7 %fusion.2 = f32[512,2048]{1,0:T(8,128)S(1)} fusion(bf16[512,768]{1,0:T(8,128)(2,1)S(1)} %get-tuple-element.5, bf16[3,2048,768]{2,1,0:T(8,128)(2,1)} %all-gather.2.cloned.1.call-done), kind=kOutput, calls=%fused_computation.10 | convolution fusion | flops 1610612736 | bytes 8126464 | tf_op jit(solution)/shard_map/dot_general | solution.py:14
  151.5 5.1 %fusion.8 = bf16[64,8,2048]{2,1,0:T(8,128)(2,1)} fusion(f32[512,2048]{1,0:T(8,128)S(1)} %fusion.2, bf16[512,768]{1,0:T(8,128)(2,1)S(1)} %get-tuple-element.4, bf16[3,2048,768]{2,1,0:T(8,128)(2,1)} %all-gather.2.cloned.1.call-done), kind=kOutput, calls=%fused_computation.18 | convolution fusion | flops 1612709888 | bytes 10223616 | tf_op jit(solution)/shard_map/dot_general | solution.py:14
  156.6 6.0 %all-to-all-start.1 = ((bf16[64,8,2048]{2,1,0:T(8,128)(2,1)}), bf16[64,8,2048]{2,1,0:T(8,128)(2,1)S(1)}, u32[]{:S(2)}, u32[]{:S(2)}) async-start(bf16[64,8,2048]{2,1,0:T(8,128)(2,1)} %fusion.8), calls=%async_computation.2 | async-start | bytes 4194304 | tf_op jit(solution)/shard_map/all_to_all | solution.py:76
  162.7 0.1 copy.18
  162.8 0.1 mul.101
  162.9 50.9 %all-to-all-done.1 = bf16[64,8,2048]{2,1,0:T(8,128)(2,1)S(1)} async-done(((bf16[64,8,2048]{2,1,0:T(8,128)(2,1)}), bf16[64,8,2048]{2,1,0:T(8,128)(2,1)S(1)}, u32[]{:S(2)}, u32[]{:S(2)}) %all-to-all-start.1) | async-done | bytes 2097184 | tf_op jit(solution)/shard_map/all_to_all | solution.py:76
  213.8 1.4 gather_fusion.1
  215.2 0.7 reshape.178
  215.9 3.6 %reduce_sum.35 = bf16[128,2048]{1,0:T(8,128)(2,1)} reduce(bf16[128,2,2048]{2,1,0:T(2,128)(2,1)S(1)} %reshape.178, bf16[]{:T(256)} %constant.42.clone.1), dimensions={1}, to_apply=%region_6.7 | reduce | flops 262144 | bytes 1572866 | tf_op jit(solution)/shard_map/reduce_sum | solution.py:78
  219.6 16.3 %reduce-scatter.2.cloned.1.call-done = bf16[3,512,768]{2,1,0:T(8,128)(2,1)} async-done(((bf16[3,2048,768]{2,1,0:T(8,128)(2,1)}), bf16[3,512,768]{2,1,0:T(8,128)(2,1)}) %reduce-scatter.2.cloned.1.call-update) | async-done | bytes 2359312 | tf_op jit(solution)/shard_map/reduce_scatter | solution.py:79
  235.9 3.9 %fusion.26 = (f32[1,512,768]{2,1,0:T(8,128)}, f32[1,512,768]{2,1,0:T(8,128)}, f32[1,512,768]{2,1,0:T(8,128)}) fusion(bf16[3,512,768]{2,1,0:T(8,128)(2,1)} %reduce-scatter.2.cloned.1.call-done), kind=kLoop, calls=%fused_computation.67 | loop fusion | bytes 9437184 | tf_op jit(solution)/shard_map/slice | solution.py:95
  (12 shorter events, 0.1 us)
Async XLA Ops:
  7.2 3.5 %copy-start.3 = (s32[128,2]{0,1:T(2,128)S(1)}, s32[128,2]{0,1:T(2,128)}, u32[]{:S(2)}) copy-start(s32[128,2]{0,1:T(2,128)} %param.9) | copy-start | bytes 3076
  7.2 5.2 %copy-start.4 = (f32[128,2]{0,1:T(2,128)S(1)}, f32[128,2]{0,1:T(2,128)}, u32[]{:S(2)}) copy-start(f32[128,2]{0,1:T(2,128)} %param.10) | copy-start | bytes 3076
  7.2 5.2 %copy-start.1 = (bf16[128,2048]{1,0:T(8,128)(2,1)S(1)}, bf16[128,2048]{1,0:T(8,128)(2,1)}, u32[]{:S(2)}) copy-start(bf16[128,2048]{1,0:T(8,128)(2,1)} %param.8) | copy-start | bytes 1572868
  7.2 119.8 %all-gather.2.cloned.1.call-start = ((), (), s32[]{:S(2)}) async-start(), calls=%async_computation.3 | async-start | bytes 11796480 | tf_op jit(solution)/shard_map/all_gather | solution.py:58
  10.6 2.1 copy-start.2
  10.6 225.3 %reduce-scatter.2.cloned.1.call-start = ((), (), s32[]{:S(2)}) async-start(), calls=%async_computation.4 | async-start | bytes 11796480 | tf_op jit(solution)/shard_map/reduce_scatter | solution.py:79
  127.0 6.4 %copy-start = (bf16[64,8,4096]{2,1,0:T(8,128)(2,1)S(1)}, bf16[64,8,4096]{2,1,0:T(8,128)(2,1)}, u32[]{:S(2)}) copy-start(bf16[64,8,4096]{2,1,0:T(8,128)(2,1)} %all_to_all.24) | copy-start | bytes 12582916
  156.6 57.3 %all-to-all-start.1 = ((bf16[64,8,2048]{2,1,0:T(8,128)(2,1)}), bf16[64,8,2048]{2,1,0:T(8,128)(2,1)S(1)}, u32[]{:S(2)}, u32[]{:S(2)}) async-start(bf16[64,8,2048]{2,1,0:T(8,128)(2,1)} %fusion.8), calls=%async_computation.2 | async-start | bytes 4194304 | tf_op jit(solution)/shard_map/all_to_all | solution.py:76
Sparse Core Ops, SparseCore 0:
  10.7 98.0 all-gather.1
  147.9 87.9 reduce-scatter.1
